TPU v7x, 256 devices: a whole 4x4x8 slice. The times are simulated.
256 devices in a mesh: node: 16 (over y, x_hi, core), tm: 16 (over z, x_lo).
Axes of the slice: x: 4 (x_hi: 2, x_lo: 2; x = x_hi * 2 + x_lo), y: 4, z: 8, core: 2. Of those that a mesh axis runs over, the one named last changes fastest.
Arguments:
- observed: bfloat16 [65536, 16384], P('node', 'tm'), may hold values from 0.5 to 32
- node_factor: bfloat16 [64, 65536], P(None, ('node', 'tm')), may hold values from 0.19921875 to 1
- time_factor: bfloat16 [64, 1024], P(None, 'tm'), may hold values from 0.19921875 to 1
- species_factor: bfloat16 [64, 16], replicated, may hold values from 0.19921875 to 1
Outputs:
- grad_node: float32 [64, 65536], P(None, ('node', 'tm'))
- grad_time: float32 [64, 1024], P(None, 'tm')
- grad_species: float32 [64, 16], replicated
All inputs are finite; a program needn't handle non-finite values.
Results may differ from a plain program's by a relative error of at most 0.0017.
Values may be sent and summed in bfloat16 or wider, within the bound.
No kernel may reach another device: no remote copies, remote signals or barrier semaphores. Data moves between devices by JAX's collectives and lax.ppermute only.
A program may use at most 64 MiB of HBM per device.

v0:
```python
import math

import jax
import jax.numpy as jnp
from jax import lax
from jax.sharding import PartitionSpec as P


def widen(values):
    return lax.optimization_barrier(values).astype(jnp.float32)


def shards(observed, node_factor, time_factor, species_factor):
    factor_rank = node_factor.shape[0]
    time_vals = time_factor.astype(jnp.float32)
    species_vals = species_factor.astype(jnp.float32)
    time_dev = time_vals.shape[1]
    species = species_vals.shape[1]
    node_rows = observed.shape[0]
    flat_width = observed.shape[1]
    khatri = (
        (time_vals[:, :, None] * species_vals[:, None, :])
        .reshape(factor_rank, flat_width)
        .astype(jnp.bfloat16)
    )
    khatri_wide = widen(khatri)
    factor_wide = lax.all_gather(node_factor, "tm", axis=1, tiled=True).astype(jnp.float32)
    modelled = lax.dot_general(
        factor_wide, khatri_wide, (((0,), (0,)), ((), ())), precision=lax.Precision.HIGHEST
    )
    derivative = ((modelled - observed.astype(jnp.float32)) / (modelled * modelled)).astype(
        jnp.bfloat16
    )
    derivative_wide = widen(derivative)
    node_part = lax.dot_general(
        khatri_wide, derivative_wide, (((1,), (1,)), ((), ())), precision=lax.Precision.HIGHEST
    )
    node_grads = node_part
    contracted = lax.dot_general(
        derivative_wide, factor_wide, (((0,), (1,)), ((), ())), precision=lax.Precision.HIGHEST
    )
    node_grads, contracted = (node_grads, contracted)
    tm_count = lax.axis_size("tm")
    steps_all = time_dev * tm_count
    nodes_all = node_rows * lax.axis_size("node")
    share_rows = node_rows // tm_count
    summed = lax.psum(node_grads, "tm")
    grad_node = lax.dynamic_slice_in_dim(summed, lax.axis_index("tm") * share_rows, share_rows, 1)
    grad_node = grad_node / math.sqrt(steps_all * species)
    by_step = contracted.reshape(time_dev, species, factor_rank)
    time_grad = jnp.einsum("tsr,rs->rt", by_step, species_vals, precision=lax.Precision.HIGHEST)
    species_grad = jnp.einsum("tsr,rt->rs", by_step, time_vals, precision=lax.Precision.HIGHEST)
    time_grad = lax.psum(time_grad, "node")
    species_grad = lax.psum(species_grad, ("node", "tm"))
    grad_time = time_grad / math.sqrt(nodes_all * species)
    grad_species = species_grad / math.sqrt(nodes_all * steps_all)
    return (grad_node, grad_time, grad_species)


def solution(mesh):
    in_specs = (P("node", "tm"), P(None, ("node", "tm")), P(None, "tm"), P())
    out_specs = (P(None, ("node", "tm")), P(None, "tm"), P())
    return jax.shard_map(shards, mesh=mesh, in_specs=in_specs, out_specs=out_specs, check_vma=False)
```

profile of v0, /device:TPU:32, one launch (start us, length us, event | category | flops | bytes accessed | tf_op | source)
XLA Modules:
  0.0 226.5 jit_solution(11420919624136938555)
XLA Ops:
  7.2 0.0 all-reduce.2.cloned.1.call-start
  7.2 0.7 convert_element_type.22
  7.9 0.8 copy.9
  8.7 0.1 multiply_convert_fusion
  8.8 36.8 %all_gather.3 = bf16[64,4096]{1,0:T(8,128)(2,1)S(1)} all-gather(bf16[64,256]{1,0:T(8,128)(2,1)} %param.5), channel_id=1, replica_groups=mesh['node'=16,'tm'=16] {'tm'}, dimensions={1}, use_global_device_ids=true | all-gather | bytes 557056 | tf_op jit(solution)/shard_map/all_gather | solution.py:27
  45.5 11.3 %copy.10 = bf16[4096,1024]{0,1:T(8,128)(2,1)} copy(bf16[4096,1024]{1,0:T(8,128)(2,1)} %param.4) | data formatting | bytes 16777216 | tf_op args[0]
  56.8 5.7 %fusion.1 = bf16[4096,1024]{0,1:T(8,128)(2,1)S(1)} fusion(bf16[4096,1024]{0,1:T(8,128)(2,1)} %copy.10, bf16[64,1024]{0,1:T(8,128)(2,1)S(1)} %bitcast.23, bf16[64,4096]{1,0:T(8,128)(2,1)S(1)} %all_gather.3), kind=kOutput, calls=%fused_computation.3 | convolution fusion | flops 557842432 | bytes 17432576 | tf_op jit(solution)/shard_map/dot_general | solution.py:28
  62.5 0.0 copy-start
  62.5 3.2 %copy-done = bf16[4096,1024]{0,1:T(8,128)(2,1)} copy-done((bf16[4096,1024]{0,1:T(8,128)(2,1)}, bf16[4096,1024]{0,1:T(8,128)(2,1)S(1)}, u32[]{:S(2)}) %copy-start) | copy-done | bytes 8388632
  65.7 2.6 %fusion.2 = f32[64,4096]{1,0:T(8,128)} fusion(bf16[64,1024]{0,1:T(8,128)(2,1)S(1)} %bitcast.24, bf16[4096,1024]{0,1:T(8,128)(2,1)S(1)} %fusion.1), kind=kOutput, calls=%fused_computation.10 | convolution fusion | flops 536870912 | bytes 9568256 | tf_op jit(solution)/shard_map/dot_general | solution.py:35
  68.3 0.0 all-reduce.2.cloned.1.call-update
  68.3 5.7 %multiply_reduce_fusion.1 = (f32[64,64]{0,1:T(8,128)S(1)}, f32[1024,64]{1,0:T(8,128)S(1)}) fusion(f32[64,16]{0,1:T(8,128)S(1)} %convert_element_type.22, bf16[4096,1024]{0,1:T(8,128)(2,1)} %copy-done, bf16[64,4096]{1,0:T(8,128)(2,1)S(1)} %all_gather.3), kind=kOutput, calls=%fused_computation.5 | convolution fusion | flops 536997888 | bytes 9195520 | tf_op jit(solution)/shard_map/dot_general | solution.py:39
  74.0 0.1 copy.18
  74.1 0.1 multiply_reduce_fusion
  74.2 76.9 %psum.23 = f32[64,16]{0,1:T(8,128)S(1)} all-reduce(f32[64,16]{0,1:T(8,128)S(1)} %multiply_reduce_fusion), channel_id=1, replica_groups=mesh['node'=16,'tm'=16] {'node','tm'}, use_global_device_ids=true, to_apply=%region_2.0 | all-reduce | flops 1024 | bytes 8192 | tf_op jit(solution)/shard_map/psum | solution.py:54
  151.1 65.8 %psum.22 = f32[64,64]{1,0:T(8,128)S(1)} all-reduce(f32[64,64]{1,0:T(8,128)S(1)} %copy.18), channel_id=1, replica_groups=mesh['node'=16,'tm'=16] {'node'}, use_global_device_ids=true, to_apply=%region_1.0 | all-reduce | flops 4096 | bytes 32768 | tf_op jit(solution)/shard_map/psum | solution.py:53
  217.0 0.6 broadcast_multiply_fusion.1
  217.6 0.6 broadcast_multiply_fusion
  218.2 0.0 all-reduce.2.cloned.1.call-done
  218.2 1.5 dynamic-slice_multiply_fusion
Async XLA Ops:
  7.2 211.0 %all-reduce.2.cloned.1.call-start = ((), (), s32[]{:S(2)}) async-start(), calls=%async_computation | async-start | bytes 2097152 | tf_op jit(solution)/shard_map/psum | solution.py:47
  62.5 3.2 %copy-start = (bf16[4096,1024]{0,1:T(8,128)(2,1)}, bf16[4096,1024]{0,1:T(8,128)(2,1)S(1)}, u32[]{:S(2)}) copy-start(bf16[4096,1024]{0,1:T(8,128)(2,1)S(1)} %fusion.1) | copy-start | bytes 25165828
Sparse Core Ops, SparseCore 0:
  68.4 138.8 all-reduce.1
where the time goes:
time: 227 us; the launch traced here: 226 us
  blocking collectives  180 us (79%)
  local copies, waits for them, and re-layouts  15.3 us (7%)
  between operations  14.1 us (6%)
  matrix products  14 us (6%)
  other arithmetic  3.56 us (2%)
    psum x1, blocking collectives, shards(): species_grad = lax.psum(species_grad, ('node', 'tm'))  76.9 us
    psum x1, blocking collectives, shards(): time_grad = lax.psum(time_grad, 'node')  65.8 us
    all_gather x1, blocking collectives, shards(): lax.all_gather(node_factor, 'tm', axis=1, tiled=True).astype(jnp.float32)  36.8 us
    unnamed x3, local copies, waits for them, and re-layouts  14.5 us
    dot_general x1, matrix products, shards(): lax.dot_general(derivative_wide, factor_wide, (((0,), (1,)), ((), ())), p...  5.71 us
    dot_general x1, matrix products, shards(): lax.dot_general(factor_wide, khatri_wide, (((0,), (0,)), ((), ())), preci...  5.67 us
  transfers between devices with their start and end apart: 1, of which 0 were waited for; matrix products, arithmetic and copies ran while one was open for 3% of the time, Pallas kernels for 0%

commit v1 on v0

v1 whole, which is shorter than its diff:
```python
import math

import jax
import jax.numpy as jnp
from jax import lax
from jax.sharding import PartitionSpec as P


def gather_blocks(values, axis):
    count = lax.axis_size(axis)
    copies = jnp.broadcast_to(values[None], (count, *values.shape))
    return lax.all_to_all(copies, axis, 0, 0, tiled=True)


def shards(observed, node_factor, time_factor, species_factor):
    factor_rank = node_factor.shape[0]
    time_vals = time_factor.astype(jnp.float32)
    species_vals = species_factor.astype(jnp.float32)
    time_dev = time_vals.shape[1]
    species = species_vals.shape[1]
    node_rows = observed.shape[0]
    flat_width = observed.shape[1]
    tm_count = lax.axis_size("tm")
    steps_all = time_dev * tm_count
    nodes_all = node_rows * lax.axis_size("node")
    share_rows = node_rows // tm_count

    khatri = (
        (time_vals[:, :, None] * species_vals[:, None, :])
        .reshape(factor_rank, flat_width)
        .astype(jnp.bfloat16)
    )
    gathered = gather_blocks(node_factor, "tm")
    factor = gathered.transpose(1, 0, 2).reshape(factor_rank, node_rows)
    modelled = lax.dot_general(
        factor, khatri, (((0,), (0,)), ((), ())), preferred_element_type=jnp.float32
    )
    derivative = ((modelled - observed.astype(jnp.float32)) / (modelled * modelled)).astype(
        jnp.bfloat16
    )
    node_part = lax.dot_general(
        khatri, derivative, (((1,), (1,)), ((), ())), preferred_element_type=jnp.float32
    )
    contracted = lax.dot_general(
        derivative, factor, (((0,), (1,)), ((), ())), preferred_element_type=jnp.float32
    )
    by_step = contracted.reshape(time_dev, species, factor_rank)
    time_part = jnp.einsum("tsr,rs->rt", by_step, species_vals, precision=lax.Precision.HIGHEST)
    species_part = jnp.einsum("tsr,rt->rs", by_step, time_vals, precision=lax.Precision.HIGHEST)

    blocks = node_part.reshape(factor_rank, tm_count, share_rows).transpose(1, 0, 2)
    riders = jnp.broadcast_to(species_part[None], (tm_count, factor_rank, species))
    payload = jnp.concatenate([blocks, riders], axis=2)
    summed = lax.all_to_all(payload, "tm", 0, 0, tiled=True).sum(0)
    grad_node = summed[:, :share_rows] / math.sqrt(steps_all * species)
    species_tm = summed[:, share_rows:]

    small = jnp.concatenate([time_part, species_tm], axis=1)
    small_sum = gather_blocks(small, "node").sum(0)
    grad_time = small_sum[:, :time_dev] / math.sqrt(nodes_all * species)
    grad_species = small_sum[:, time_dev:] / math.sqrt(nodes_all * steps_all)
    return (grad_node, grad_time, grad_species)


def solution(mesh):
    in_specs = (P("node", "tm"), P(None, ("node", "tm")), P(None, "tm"), P())
    out_specs = (P(None, ("node", "tm")), P(None, "tm"), P())
    return jax.shard_map(shards, mesh=mesh, in_specs=in_specs, out_specs=out_specs, check_vma=False)
```

time: 227 us -> 129 us (0.57)
  the two profiles are of different devices: /device:TPU:32 before, /device:TPU:1 now
where the time goes in v1:
time: 129 us; the launch traced here: 128 us
  waiting for transfers between devices  49.2 us (38%)
  local copies, waits for them, and re-layouts  28.2 us (22%)
  starting transfers between devices  26.1 us (20%)
  matrix products  19.9 us (15%)
  other arithmetic  3.6 us (3%)
    all_to_all x1, waiting for transfers between devices, shards(): summed = lax.all_to_all(payload, 'tm', 0, 0, tiled=True).sum(0)  35.8 us
    all_to_all x2, starting transfers between devices, gather_blocks(): return lax.all_to_all(copies, axis, 0, 0, tiled=True)  21.4 us
    all_to_all x2, waiting for transfers between devices, gather_blocks(): return lax.all_to_all(copies, axis, 0, 0, tiled=True)  13.4 us
    unnamed x4, local copies, waits for them, and re-layouts  11.9 us
    dot_general x1, local copies, waits for them, and re-layouts, shards(): lax.dot_general(khatri, derivative, (((1,), (1,)), ((), ())), preferred_e...  11.9 us
    dot_general x1, matrix products, shards(): lax.dot_general(factor, khatri, (((0,), (0,)), ((), ())), preferred_eleme...  7.57 us
    dot_general x1, matrix products, shards(): lax.dot_general(khatri, derivative, (((1,), (1,)), ((), ())), preferred_e...  6.05 us
    dot_general x1, matrix products, shards(): lax.dot_general(derivative, factor, (((0,), (1,)), ((), ())), preferred_e...  5.72 us
  transfers between devices with their start and end apart: 3, of which 3 were waited for; matrix products, arithmetic and copies ran while one was open for 11% of the time, Pallas kernels for 0%

profile of v1, /device:TPU:1, one launch (start us, length us, event | category | flops | bytes accessed | tf_op | source)
XLA Modules:
  0.0 127.7 jit_solution(11698297155095914532)
XLA Ops:
  0.6 1.7 %broadcast_in_dim.6 = bf16[16,64,256]{2,1,0:T(8,128)(2,1)} broadcast(bf16[64,256]{1,0:T(8,128)(2,1)} %param.5), dimensions={1,2} | broadcast | bytes 557056 | tf_op jit(solution)/shard_map/broadcast_in_dim | solution.py:11
  2.3 10.0 %all-to-all-start = ((bf16[16,64,256]{2,1,0:T(8,128)(2,1)}), bf16[16,64,256]{2,1,0:T(8,128)(2,1)S(1)}, u32[]{:S(2)}, u32[]{:S(2)}) async-start(bf16[16,64,256]{2,1,0:T(8,128)(2,1)} %broadcast_in_dim.6), calls=%async_computation | async-start | bytes 1048576 | tf_op jit(solution)/shard_map/all_to_all | solution.py:12
  12.3 0.7 convert_element_type.29
  13.0 0.8 copy.22
  13.8 11.3 %copy.24 = bf16[4096,1024]{0,1:T(8,128)(2,1)} copy(bf16[4096,1024]{1,0:T(8,128)(2,1)} %param.4) | data formatting | bytes 16777216 | tf_op args[0]
  25.1 2.9 %all-to-all-done = bf16[16,64,256]{2,1,0:T(8,128)(2,1)S(1)} async-done(((bf16[16,64,256]{2,1,0:T(8,128)(2,1)}), bf16[16,64,256]{2,1,0:T(8,128)(2,1)S(1)}, u32[]{:S(2)}, u32[]{:S(2)}) %all-to-all-start) | async-done | bytes 524320 | tf_op jit(solution)/shard_map/all_to_all | solution.py:12
  28.0 0.3 copy.23
  28.3 0.2 reshape.37
  28.6 7.6 %fusion.1 = bf16[4096,1024]{0,1:T(8,128)(2,1)} fusion(bf16[4096,1024]{0,1:T(8,128)(2,1)} %copy.24, bf16[64,1024]{0,1:T(8,128)(2,1)S(1)} %bitcast.37, bf16[64,4096]{1,0:T(8,128)(2,1)S(1)} %bitcast.39), kind=kOutput, calls=%fused_computation.3 | convolution fusion | flops 557842432 | bytes 17432576 | tf_op jit(solution)/shard_map/dot_general | solution.py:35
  36.2 11.9 %copy.38 = bf16[4096,1024]{1,0:T(8,128)(2,1)} copy(bf16[4096,1024]{0,1:T(8,128)(2,1)} %fusion.1) | data formatting | bytes 16777216 | tf_op jit(solution)/shard_map/dot_general | solution.py:41
  48.1 0.0 copy-start
  48.1 5.7 %multiply_reduce_fusion = (f32[64,64]{0,1:T(8,128)S(1)}, f32[64,16,64]{2,1,0:T(8,128)S(1)}) fusion(f32[64,16]{0,1:T(8,128)S(1)} %convert_element_type.29, bf16[64,16,4096]{2,1,0:T(8,128)(2,1)} %bitcast.34, bf16[64,4096,1]{1,0,2:T(8,128)(2,1)S(1)} %reshape.37), kind=kOutput, calls=%fused_computation.6 | convolution fusion | flops 536997888 | bytes 9195520 | tf_op jit(solution)/shard_map/dot_general | solution.py:44
  53.8 0.4 copy.29
  54.2 0.0 copy-done
  54.2 0.5 fusion.2
  54.8 6.1 %convolution_bitcast_fusion = f32[16,64,256]{2,1,0:T(8,128)S(1)} fusion(bf16[64,1024,1]{0,1,2:T(8,128)(2,1)S(1)} %bitcast.38, bf16[16,256,1024]{2,1,0:T(8,128)(2,1)} %bitcast.33), kind=kOutput, calls=%fused_computation.5 | convolution fusion | flops 536870912 | bytes 9568256 | tf_op jit(solution)/shard_map/dot_general | solution.py:41
  60.8 0.1 broadcast_in_dim.7
  60.9 1.3 %pad_maximum_fusion = f32[16,64,272]{2,1,0:T(8,128)} fusion(f32[16,64,16]{2,1,0:T(8,128)S(1)} %broadcast_in_dim.7, f32[16,64,256]{2,1,0:T(8,128)S(1)} %convolution_bitcast_fusion), kind=kLoop, calls=%fused_computation.4 | loop fusion | flops 278528 | bytes 2228224 | tf_op jit(solution)/shard_map/concatenate | solution.py:53
  62.2 4.7 %all-to-all-start.1 = ((f32[16,64,272]{2,1,0:T(8,128)}), f32[16,64,272]{2,1,0:T(8,128)S(1)}, u32[]{:S(2)}, u32[]{:S(2)}) async-start(f32[16,64,272]{2,1,0:T(8,128)} %pad_maximum_fusion), calls=%async_computation.1 | async-start | bytes 3145728 | tf_op jit(solution)/shard_map/all_to_all | solution.py:54
  66.9 0.1 copy.36
  67.0 35.8 %all-to-all-done.1 = f32[16,64,272]{2,1,0:T(8,128)S(1)} async-done(((f32[16,64,272]{2,1,0:T(8,128)}), f32[16,64,272]{2,1,0:T(8,128)S(1)}, u32[]{:S(2)}, u32[]{:S(2)}) %all-to-all-start.1) | async-done | bytes 1114144 | tf_op jit(solution)/shard_map/all_to_all | solution.py:54
  102.8 0.1 reduce_sum.18
  102.9 0.1 pad_maximum_fusion.1
  103.0 0.8 broadcast_in_dim.8
  103.8 11.4 %all-to-all-start.2 = ((f32[16,64,80]{2,1,0:T(8,128)}), f32[16,64,80]{2,1,0:T(8,128)S(1)}, u32[]{:S(2)}, u32[]{:S(2)}) async-start(f32[16,64,80]{2,1,0:T(8,128)} %broadcast_in_dim.8), calls=%async_computation.2 | async-start | bytes 1048576 | tf_op jit(solution)/shard_map/all_to_all | solution.py:12
  115.2 0.6 slice_multiply_fusion
  115.8 10.5 %all-to-all-done.2 = f32[16,64,80]{2,1,0:T(8,128)S(1)} async-done(((f32[16,64,80]{2,1,0:T(8,128)}), f32[16,64,80]{2,1,0:T(8,128)S(1)}, u32[]{:S(2)}, u32[]{:S(2)}) %all-to-all-start.2) | async-done | bytes 327712 | tf_op jit(solution)/shard_map/all_to_all | solution.py:12
  126.4 0.1 slice_multiply_fusion.1
  126.5 0.6 slice_multiply_fusion.2
  127.1 0.7 copy.27
  (4 shorter events, 0.1 us)
Async XLA Ops:
  2.3 25.7 %all-to-all-start = ((bf16[16,64,256]{2,1,0:T(8,128)(2,1)}), bf16[16,64,256]{2,1,0:T(8,128)(2,1)S(1)}, u32[]{:S(2)}, u32[]{:S(2)}) async-start(bf16[16,64,256]{2,1,0:T(8,128)(2,1)} %broadcast_in_dim.6), calls=%async_computation | async-start | bytes 1048576 | tf_op jit(solution)/shard_map/all_to_all | solution.py:12
  48.1 6.1 %copy-start = (bf16[64,64]{1,0:T(8,128)(2,1)S(1)}, bf16[64,64]{1,0:T(8,128)(2,1)}, u32[]{:S(2)}) copy-start(bf16[64,64]{1,0:T(8,128)(2,1)} %param.6) | copy-start | bytes 24580
  62.2 40.6 %all-to-all-start.1 = ((f32[16,64,272]{2,1,0:T(8,128)}), f32[16,64,272]{2,1,0:T(8,128)S(1)}, u32[]{:S(2)}, u32[]{:S(2)}) async-start(f32[16,64,272]{2,1,0:T(8,128)} %pad_maximum_fusion), calls=%async_computation.1 | async-start | bytes 3145728 | tf_op jit(solution)/shard_map/all_to_all | solution.py:54
  103.8 22.5 %all-to-all-start.2 = ((f32[16,64,80]{2,1,0:T(8,128)}), f32[16,64,80]{2,1,0:T(8,128)S(1)}, u32[]{:S(2)}, u32[]{:S(2)}) async-start(f32[16,64,80]{2,1,0:T(8,128)} %broadcast_in_dim.8), calls=%async_computation.2 | async-start | bytes 1048576 | tf_op jit(solution)/shard_map/all_to_all | solution.py:12

commit v2 on v1

--- a/solution.py
+++ b/solution.py
@@ -3,7 +3,57 @@
 import jax
 import jax.numpy as jnp
 from jax import lax
+from jax.experimental import pallas as pl
+from jax.experimental.pallas import tpu as pltpu
 from jax.sharding import PartitionSpec as P
+
+ROW_TILE = 512
+
+
+def fused_kernel(obs_ref, factor_t_ref, factor_ref, khatri_ref, node_ref, contracted_ref):
+    step = pl.program_id(0)
+    khatri = khatri_ref[...]
+    modelled = jnp.dot(factor_t_ref[...], khatri, preferred_element_type=jnp.float32)
+    derivative = ((modelled - obs_ref[...].astype(jnp.float32)) / (modelled * modelled)).astype(
+        jnp.bfloat16
+    )
+    node_ref[...] = lax.dot_general(
+        khatri, derivative, (((1,), (1,)), ((), ())), preferred_element_type=jnp.float32
+    )
+    part = jnp.dot(factor_ref[...], derivative, preferred_element_type=jnp.float32)
+
+    @pl.when(step == 0)
+    def _():
+        contracted_ref[...] = part
+
+    @pl.when(step > 0)
+    def _():
+        contracted_ref[...] += part
+
+
+def fused(observed, factor_t, factor, khatri):
+    rows, width = observed.shape
+    rank = factor.shape[0]
+    tile = min(ROW_TILE, rows)
+    return pl.pallas_call(
+        fused_kernel,
+        grid=(rows // tile,),
+        in_specs=[
+            pl.BlockSpec((tile, width), lambda i: (i, 0)),
+            pl.BlockSpec((tile, rank), lambda i: (i, 0)),
+            pl.BlockSpec((rank, tile), lambda i: (0, i)),
+            pl.BlockSpec((rank, width), lambda i: (0, 0)),
+        ],
+        out_specs=[
+            pl.BlockSpec((rank, tile), lambda i: (0, i)),
+            pl.BlockSpec((rank, width), lambda i: (0, 0)),
+        ],
+        out_shape=[
+            jax.ShapeDtypeStruct((rank, rows), jnp.float32),
+            jax.ShapeDtypeStruct((rank, width), jnp.float32),
+        ],
+        compiler_params=pltpu.CompilerParams(dimension_semantics=("arbitrary",)),
+    )(observed, factor_t, factor, khatri)
 
 
 def gather_blocks(values, axis):
@@ -32,21 +82,11 @@
     )
     gathered = gather_blocks(node_factor, "tm")
     factor = gathered.transpose(1, 0, 2).reshape(factor_rank, node_rows)
-    modelled = lax.dot_general(
-        factor, khatri, (((0,), (0,)), ((), ())), preferred_element_type=jnp.float32
-    )
-    derivative = ((modelled - observed.astype(jnp.float32)) / (modelled * modelled)).astype(
-        jnp.bfloat16
-    )
-    node_part = lax.dot_general(
-        khatri, derivative, (((1,), (1,)), ((), ())), preferred_element_type=jnp.float32
-    )
-    contracted = lax.dot_general(
-        derivative, factor, (((0,), (1,)), ((), ())), preferred_element_type=jnp.float32
-    )
-    by_step = contracted.reshape(time_dev, species, factor_rank)
-    time_part = jnp.einsum("tsr,rs->rt", by_step, species_vals, precision=lax.Precision.HIGHEST)
-    species_part = jnp.einsum("tsr,rt->rs", by_step, time_vals, precision=lax.Precision.HIGHEST)
+    factor_t = gathered.transpose(0, 2, 1).reshape(node_rows, factor_rank)
+    node_part, contracted_t = fused(observed, factor_t, factor, khatri)
+    by_step = contracted_t.reshape(factor_rank, time_dev, species)
+    time_part = (by_step * species_vals[:, None, :]).sum(2)
+    species_part = (by_step * time_vals[:, :, None]).sum(1)
 
     blocks = node_part.reshape(factor_rank, tm_count, share_rows).transpose(1, 0, 2)
     riders = jnp.broadcast_to(species_part[None], (tm_count, factor_rank, species))

time: 129 us -> 111 us (0.86)
  local copies, waits for them, and re-layouts: 28.2 us -> 8.02 us
  matrix products: 19.9 us -> 0 us
  waiting for transfers between devices: 49.2 us -> 61 us
  Pallas kernels: 0 us -> 11 us
    dot_general x4 -> x0, matrix products: 19.9 us -> none  [the longest x1 7.57 us: shards(): lax.dot_general(factor, khatri, (((0,), (0,)), ((), ())), preferred_eleme...]
    dot_general x3 -> x0, local copies, waits for them, and re-layouts: 12.4 us -> none  [the longest x1 11.9 us: shards(): lax.dot_general(khatri, derivative, (((1,), (1,)), ((), ())), preferred_e...]
    all_to_all x2, waiting for transfers between devices: 13.4 us -> 25.3 us  [gather_blocks(): return lax.all_to_all(copies, axis, 0, 0, tiled=True)]
    unnamed x4 -> x7, local copies, waits for them, and re-layouts: 11.9 us -> 0.68 us
    pallas_call x0 -> x1, Pallas kernels: none -> 11 us  [fused(): pl.pallas_call(fused_kernel, grid=(rows // tile,), in_specs=[pl.BlockSpec...]
    reshape x0 -> x1, local copies, waits for them, and re-layouts: none -> 1.37 us  [shards(): node_part.reshape(factor_rank, tm_count, share_rows).transpose(1, 0, 2)]
  transfers between devices with their start and end apart: 3 -> 3, of which waited for: 3 -> 3; matrix products, arithmetic and copies ran while one was open for 11% -> 2% of each run, Pallas kernels for 0% -> 0%
where the time goes in v2:
time: 111 us; the launch traced here: 110 us
  waiting for transfers between devices  61 us (55%)
  starting transfers between devices  26.1 us (24%)
  Pallas kernels  11 us (10%)
  local copies, waits for them, and re-layouts  8.02 us (7%)
  other arithmetic  3.05 us (3%)
    all_to_all x1, waiting for transfers between devices, shards(): summed = lax.all_to_all(payload, 'tm', 0, 0, tiled=True).sum(0)  35.8 us
    all_to_all x2, waiting for transfers between devices, gather_blocks(): return lax.all_to_all(copies, axis, 0, 0, tiled=True)  25.3 us
    all_to_all x2, starting transfers between devices, gather_blocks(): return lax.all_to_all(copies, axis, 0, 0, tiled=True)  21.4 us
    pallas_call x1, Pallas kernels, fused(): pl.pallas_call(fused_kernel, grid=(rows // tile,), in_specs=[pl.BlockSpec...  11 us
    all_to_all x1, starting transfers between devices, shards(): summed = lax.all_to_all(payload, 'tm', 0, 0, tiled=True).sum(0)  4.71 us
    broadcast_in_dim x2, local copies, waits for them, and re-layouts, gather_blocks(): copies = jnp.broadcast_to(values[None], (count, *values.shape))  2.47 us
  transfers between devices with their start and end apart: 3, of which 3 were waited for; matrix products, arithmetic and copies ran while one was open for 2% of the time, Pallas kernels for 0%

profile of v2, /device:TPU:1, one launch (start us, length us, event | category | flops | bytes accessed | tf_op | source)
XLA Modules:
  0.0 109.9 jit_solution(12409062582743601942)
XLA Ops:
  0.6 0.0 copy-start.2
  0.6 0.0 copy-start.1
  0.7 1.6 %broadcast_in_dim.6 = bf16[16,64,256]{2,1,0:T(8,128)(2,1)} broadcast(bf16[64,256]{1,0:T(8,128)(2,1)} %param.5), dimensions={1,2} | broadcast | bytes 557056 | tf_op jit(solution)/shard_map/broadcast_in_dim | solution.py:61
  2.3 10.0 %all-to-all-start = ((bf16[16,64,256]{2,1,0:T(8,128)(2,1)}), bf16[16,64,256]{2,1,0:T(8,128)(2,1)S(1)}, u32[]{:S(2)}, u32[]{:S(2)}) async-start(bf16[16,64,256]{2,1,0:T(8,128)(2,1)} %broadcast_in_dim.6), calls=%async_computation | async-start | bytes 1048576 | tf_op jit(solution)/shard_map/all_to_all | solution.py:62
  12.3 0.0 copy-done.2
  12.3 0.0 copy-done.1
  12.3 0.1 copy.37
  12.4 0.1 multiply_convert_fusion
  12.5 0.8 copy.38.khatri_ref
  13.3 14.8 %all-to-all-done = bf16[16,64,256]{2,1,0:T(8,128)(2,1)S(1)} async-done(((bf16[16,64,256]{2,1,0:T(8,128)(2,1)}), bf16[16,64,256]{2,1,0:T(8,128)(2,1)S(1)}, u32[]{:S(2)}, u32[]{:S(2)}) %all-to-all-start) | async-done | bytes 524320 | tf_op jit(solution)/shard_map/all_to_all | solution.py:62
  28.0 0.8 copy.46
  28.8 1.3 %copy.35 = bf16[16,256,64]{2,1,0:T(8,128)(2,1)} copy(bf16[16,256,64]{1,2,0:T(8,128)(2,1)S(1)} %bitcast.16) | data formatting | bytes 1048576 | tf_op jit(solution)/shard_map/transpose | solution.py:85
  30.2 11.0 %shard_map.67 = (f32[64,4096]{1,0:T(8,128)}, f32[64,1024]{1,0:T(8,128)}) custom-call(bf16[4096,1024]{1,0:T(8,128)(2,1)} %obs_ref.1, bf16[4096,64]{1,0:T(8,128)(2,1)} %bitcast.19, bf16[64,4096]{1,0:T(8,128)(2,1)} %bitcast.20, bf16[64,1024]{1,0:T(8,128)(2,1)} %copy.38.khatri_ref), custom_call_target="tpu_custom_call" | custom-call | tf_op jit(solution)/shard_map/pallas_call | solution.py:38
  41.1 1.4 %copy.48 = f32[8,16,8,256]{3,2,0,1:T(8,128)S(1)} copy(f32[8,16,8,256]{3,2,1,0:T(8,128)} %bitcast.22) | data formatting | bytes 2097152 | tf_op jit(solution)/shard_map/reshape | solution.py:91
  42.5 0.2 copy.40
  42.7 0.1 multiply_reduce_fusion.1
  42.8 0.1 copy.41
  42.9 0.1 broadcast_in_dim.7
  43.0 1.3 %pad_maximum_fusion = f32[16,64,272]{2,1,0:T(8,128)} fusion(f32[16,64,16]{2,1,0:T(8,128)S(1)} %broadcast_in_dim.7, f32[16,64,256]{2,1,0:T(8,128)S(1)} %bitcast.18), kind=kLoop, calls=%fused_computation | loop fusion | flops 278528 | bytes 2228224 | tf_op jit(solution)/shard_map/concatenate | solution.py:93
  44.3 4.7 %all-to-all-start.1 = ((f32[16,64,272]{2,1,0:T(8,128)}), f32[16,64,272]{2,1,0:T(8,128)S(1)}, u32[]{:S(2)}, u32[]{:S(2)}) async-start(f32[16,64,272]{2,1,0:T(8,128)} %pad_maximum_fusion), calls=%async_computation.1 | async-start | bytes 3145728 | tf_op jit(solution)/shard_map/all_to_all | solution.py:94
  49.0 0.1 multiply_reduce_fusion
  49.1 35.8 %all-to-all-done.1 = f32[16,64,272]{2,1,0:T(8,128)S(1)} async-done(((f32[16,64,272]{2,1,0:T(8,128)}), f32[16,64,272]{2,1,0:T(8,128)S(1)}, u32[]{:S(2)}, u32[]{:S(2)}) %all-to-all-start.1) | async-done | bytes 1114144 | tf_op jit(solution)/shard_map/all_to_all | solution.py:94
  84.9 0.1 reduce_sum.37
  85.0 0.1 copy.42
  85.0 0.1 copy.43
  85.1 0.9 broadcast_in_dim.8
  86.0 11.3 %all-to-all-start.2 = ((f32[16,64,80]{2,1,0:T(8,128)}), f32[16,64,80]{2,1,0:T(8,128)S(1)}, u32[]{:S(2)}, u32[]{:S(2)}) async-start(f32[16,64,80]{2,1,0:T(8,128)} %broadcast_in_dim.8), calls=%async_computation.2 | async-start | bytes 1048576 | tf_op jit(solution)/shard_map/all_to_all | solution.py:62
  97.3 0.6 slice_multiply_fusion
  98.0 10.5 %all-to-all-done.2 = f32[16,64,80]{2,1,0:T(8,128)S(1)} async-done(((f32[16,64,80]{2,1,0:T(8,128)}), f32[16,64,80]{2,1,0:T(8,128)S(1)}, u32[]{:S(2)}, u32[]{:S(2)}) %all-to-all-start.2) | async-done | bytes 327712 | tf_op jit(solution)/shard_map/all_to_all | solution.py:62
  108.5 0.1 slice_multiply_fusion.1
  108.6 0.6 slice_multiply_fusion.2
  109.2 0.7 copy.44
  (6 shorter events, 0.1 us)
Async XLA Ops:
  0.6 11.7 %copy-start.2 = (bf16[64,16]{0,1:T(8,128)(2,1)S(1)}, bf16[64,16]{0,1:T(8,128)(2,1)}, u32[]{:S(2)}) copy-start(bf16[64,16]{0,1:T(8,128)(2,1)} %param.7) | copy-start | bytes 6148
  0.6 11.7 %copy-start.1 = (bf16[64,64]{1,0:T(8,128)(2,1)S(1)}, bf16[64,64]{1,0:T(8,128)(2,1)}, u32[]{:S(2)}) copy-start(bf16[64,64]{1,0:T(8,128)(2,1)} %param.6) | copy-start | bytes 24580
  2.3 25.7 %all-to-all-start = ((bf16[16,64,256]{2,1,0:T(8,128)(2,1)}), bf16[16,64,256]{2,1,0:T(8,128)(2,1)S(1)}, u32[]{:S(2)}, u32[]{:S(2)}) async-start(bf16[16,64,256]{2,1,0:T(8,128)(2,1)} %broadcast_in_dim.6), calls=%async_computation | async-start | bytes 1048576 | tf_op jit(solution)/shard_map/all_to_all | solution.py:62
  41.1 1.4 %copy-start = (f32[64,1024]{1,0:T(8,128)S(1)}, f32[64,1024]{1,0:T(8,128)}, u32[]{:S(2)}) copy-start(f32[64,1024]{1,0:T(8,128)} %get-tuple-element.6) | copy-start | bytes 786436
  44.3 40.6 %all-to-all-start.1 = ((f32[16,64,272]{2,1,0:T(8,128)}), f32[16,64,272]{2,1,0:T(8,128)S(1)}, u32[]{:S(2)}, u32[]{:S(2)}) async-start(f32[16,64,272]{2,1,0:T(8,128)} %pad_maximum_fusion), calls=%async_computation.1 | async-start | bytes 3145728 | tf_op jit(solution)/shard_map/all_to_all | solution.py:94
  86.0 22.5 %all-to-all-start.2 = ((f32[16,64,80]{2,1,0:T(8,128)}), f32[16,64,80]{2,1,0:T(8,128)S(1)}, u32[]{:S(2)}, u32[]{:S(2)}) async-start(f32[16,64,80]{2,1,0:T(8,128)} %broadcast_in_dim.8), calls=%async_computation.2 | async-start | bytes 1048576 | tf_op jit(solution)/shard_map/all_to_all | solution.py:62

commit v3 on v2

--- a/solution.py
+++ b/solution.py
@@ -62,6 +62,15 @@
     return lax.all_to_all(copies, axis, 0, 0, tiled=True)
 
 
+def butterfly_sum(values, axis):
+    count = lax.axis_size(axis)
+    rounds = count.bit_length() - 1
+    for k in range(rounds):
+        pairs = [(i, i ^ (1 << k)) for i in range(count)]
+        values = values + lax.ppermute(values, axis, pairs)
+    return values
+
+
 def shards(observed, node_factor, time_factor, species_factor):
     factor_rank = node_factor.shape[0]
     time_vals = time_factor.astype(jnp.float32)
@@ -88,17 +97,15 @@
     time_part = (by_step * species_vals[:, None, :]).sum(2)
     species_part = (by_step * time_vals[:, :, None]).sum(1)
 
+    small = jnp.concatenate([time_part, species_part], axis=1)
+    small_sum = butterfly_sum(small, "node")
+    grad_time = small_sum[:, :time_dev] / math.sqrt(nodes_all * species)
+    species_sum = butterfly_sum(small_sum[:, time_dev:], "tm")
+    grad_species = species_sum / math.sqrt(nodes_all * steps_all)
+
     blocks = node_part.reshape(factor_rank, tm_count, share_rows).transpose(1, 0, 2)
-    riders = jnp.broadcast_to(species_part[None], (tm_count, factor_rank, species))
-    payload = jnp.concatenate([blocks, riders], axis=2)
-    summed = lax.all_to_all(payload, "tm", 0, 0, tiled=True).sum(0)
-    grad_node = summed[:, :share_rows] / math.sqrt(steps_all * species)
-    species_tm = summed[:, share_rows:]
-
-    small = jnp.concatenate([time_part, species_tm], axis=1)
-    small_sum = gather_blocks(small, "node").sum(0)
-    grad_time = small_sum[:, :time_dev] / math.sqrt(nodes_all * species)
-    grad_species = small_sum[:, time_dev:] / math.sqrt(nodes_all * steps_all)
+    summed = lax.all_to_all(blocks, "tm", 0, 0, tiled=True).sum(0)
+    grad_node = summed / math.sqrt(steps_all * species)
     return (grad_node, grad_time, grad_species)
 
 

time: 111 us -> 90.9 us (0.82)
  the two profiles are of different devices: /device:TPU:1 before, /device:TPU:22 now
where the time goes in v3:
time: 90.9 us; the launch traced here: 90.2 us
  waiting for transfers between devices  38 us (42%)
  starting transfers between devices  28.7 us (32%)
  Pallas kernels  11 us (12%)
  local copies, waits for them, and re-layouts  9.57 us (11%)
  other arithmetic  2.26 us (2%)
    ppermute x8, waiting for transfers between devices, butterfly_sum(): values = values + lax.ppermute(values, axis, pairs)  25 us
    ppermute x8, starting transfers between devices, butterfly_sum(): values = values + lax.ppermute(values, axis, pairs)  13.2 us
    all_to_all x1, waiting for transfers between devices, gather_blocks(): return lax.all_to_all(copies, axis, 0, 0, tiled=True)  12.9 us
    pallas_call x1, Pallas kernels, fused(): pl.pallas_call(fused_kernel, grid=(rows // tile,), in_specs=[pl.BlockSpec...  11 us
    all_to_all x1, starting transfers between devices, gather_blocks(): return lax.all_to_all(copies, axis, 0, 0, tiled=True)  9.94 us
    all_to_all x1, starting transfers between devices, shards(): summed = lax.all_to_all(blocks, 'tm', 0, 0, tiled=True).sum(0)  5.59 us
    reshape x1, local copies, waits for them, and re-layouts, shards(): node_part.reshape(factor_rank, tm_count, share_rows).transpose(1, 0, 2)  2.36 us
  transfers between devices with their start and end apart: 10, of which 9 were waited for; matrix products, arithmetic and copies ran while one was open for 6% of the time, Pallas kernels for 0%

profile of v3, /device:TPU:22, one launch (start us, length us, event | category | flops | bytes accessed | tf_op | source)
XLA Modules:
  0.0 90.2 jit_solution(10094997264484401115)
XLA Ops:
  0.6 1.6 %broadcast_in_dim.2 = bf16[16,64,256]{2,1,0:T(8,128)(2,1)} broadcast(bf16[64,256]{1,0:T(8,128)(2,1)} %param.5), dimensions={1,2} | broadcast | bytes 557056 | tf_op jit(solution)/shard_map/broadcast_in_dim | solution.py:61
  2.2 9.9 %all-to-all-start = ((bf16[16,64,256]{2,1,0:T(8,128)(2,1)}), bf16[16,64,256]{2,1,0:T(8,128)(2,1)S(1)}, u32[]{:S(2)}, u32[]{:S(2)}) async-start(bf16[16,64,256]{2,1,0:T(8,128)(2,1)} %broadcast_in_dim.2), calls=%async_computation | async-start | bytes 1048576 | tf_op jit(solution)/shard_map/all_to_all | solution.py:62
  12.2 0.7 convert_element_type.12
  12.9 0.8 copy.17
  13.7 0.8 copy.18.khatri_ref
  14.5 12.9 %all-to-all-done = bf16[16,64,256]{2,1,0:T(8,128)(2,1)S(1)} async-done(((bf16[16,64,256]{2,1,0:T(8,128)(2,1)}), bf16[16,64,256]{2,1,0:T(8,128)(2,1)S(1)}, u32[]{:S(2)}, u32[]{:S(2)}) %all-to-all-start) | async-done | bytes 524320 | tf_op jit(solution)/shard_map/all_to_all | solution.py:62
  27.4 0.8 copy.23
  28.2 1.4 %copy.15 = bf16[16,256,64]{2,1,0:T(8,128)(2,1)} copy(bf16[16,256,64]{1,2,0:T(8,128)(2,1)S(1)} %bitcast.16) | data formatting | bytes 1048576 | tf_op jit(solution)/shard_map/transpose | solution.py:94
  29.6 11.0 %shard_map.67 = (f32[64,4096]{1,0:T(8,128)}, f32[64,1024]{1,0:T(8,128)}) custom-call(bf16[4096,1024]{1,0:T(8,128)(2,1)} %obs_ref.1, bf16[4096,64]{1,0:T(8,128)(2,1)} %bitcast.18, bf16[64,4096]{1,0:T(8,128)(2,1)} %bitcast.19, bf16[64,1024]{1,0:T(8,128)(2,1)} %copy.18.khatri_ref), custom_call_target="tpu_custom_call" | custom-call | tf_op jit(solution)/shard_map/pallas_call | solution.py:38
  40.6 2.4 %copy.25 = f32[8,16,8,256]{3,2,0,1:T(8,128)} copy(f32[8,16,8,256]{3,2,1,0:T(8,128)} %bitcast.21) | data formatting | bytes 2097152 | tf_op jit(solution)/shard_map/reshape | solution.py:106
  42.9 5.6 %all-to-all-start.1 = ((f32[16,64,256]{2,1,0:T(8,128)}), f32[16,64,256]{2,1,0:T(8,128)S(1)}, u32[]{:S(2)}, u32[]{:S(2)}) async-start(f32[16,64,256]{2,1,0:T(8,128)} %bitcast.14), calls=%async_computation.1 | async-start | bytes 2097152 | tf_op jit(solution)/shard_map/all_to_all | solution.py:107
  48.5 1.1 %copy.20 = f32[64,1024]{0,1:T(8,128)S(1)} copy(f32[64,1024]{1,0:T(8,128)} %get-tuple-element.6) | data formatting | bytes 524288 | tf_op jit(solution)/shard_map/pallas_call | solution.py:38
  49.7 0.2 multiply_reduce_fusion
  49.9 0.1 collective-permute-start
  50.0 1.2 %collective-permute-done = f32[64,80]{0,1:T(8,128)S(1)} collective-permute-done((f32[64,80]{0,1:T(8,128)S(1)}, f32[64,80]{0,1:T(8,128)S(1)}, u32[]{:S(2)}, u32[]{:S(2)}) %collective-permute-start) | collective-permute-done | bytes 20512 | tf_op jit(solution)/shard_map/ppermute | solution.py:70
  51.2 1.5 %collective-permute-start.1 = (f32[64,80]{0,1:T(8,128)S(1)}, f32[64,80]{0,1:T(8,128)S(1)}, u32[]{:S(2)}, u32[]{:S(2)}) collective-permute-start(f32[64,80]{0,1:T(8,128)S(1)} %fusion), channel_id=1, source_target_pairs={{0,32},{16,48},{32,0},{48,16},{64,96},{80,112},{96,64},{112,80},{1... | collective-permute-start | bytes 61448 | tf_op jit(solution)/shard_map/ppermute | solution.py:70
  52.7 4.3 %collective-permute-done.1 = f32[64,80]{0,1:T(8,128)S(1)} collective-permute-done((f32[64,80]{0,1:T(8,128)S(1)}, f32[64,80]{0,1:T(8,128)S(1)}, u32[]{:S(2)}, u32[]{:S(2)}) %collective-permute-start.1) | collective-permute-done | bytes 20512 | tf_op jit(solution)/shard_map/ppermute | solution.py:70
  57.0 1.3 %collective-permute-start.2 = (f32[64,80]{0,1:T(8,128)S(1)}, f32[64,80]{0,1:T(8,128)S(1)}, u32[]{:S(2)}, u32[]{:S(2)}) collective-permute-start(f32[64,80]{0,1:T(8,128)S(1)} %add.25), channel_id=1, source_target_pairs={{0,64},{16,80},{32,96},{48,112},{64,0},{80,16},{96,32},{112,48},{1... | collective-permute-start | bytes 61448 | tf_op jit(solution)/shard_map/ppermute | solution.py:70
  58.3 2.7 %collective-permute-done.2 = f32[64,80]{0,1:T(8,128)S(1)} collective-permute-done((f32[64,80]{0,1:T(8,128)S(1)}, f32[64,80]{0,1:T(8,128)S(1)}, u32[]{:S(2)}, u32[]{:S(2)}) %collective-permute-start.2) | collective-permute-done | bytes 20512 | tf_op jit(solution)/shard_map/ppermute | solution.py:70
  61.0 0.3 collective-permute-start.3
  61.4 5.2 %collective-permute-done.3 = f32[64,80]{0,1:T(8,128)S(1)} collective-permute-done((f32[64,80]{0,1:T(8,128)S(1)}, f32[64,80]{0,1:T(8,128)S(1)}, u32[]{:S(2)}, u32[]{:S(2)}) %collective-permute-start.3) | collective-permute-done | bytes 20512 | tf_op jit(solution)/shard_map/ppermute | solution.py:70
  66.5 0.2 collective-permute-start.4
  66.8 4.0 %collective-permute-done.4 = f32[64,16]{0,1:T(8,128)S(1)} collective-permute-done((f32[64,16]{0,1:T(8,128)S(1)}, f32[64,16]{0,1:T(8,128)S(1)}, u32[]{:S(2)}, u32[]{:S(2)}) %collective-permute-start.4) | collective-permute-done | bytes 4128 | tf_op jit(solution)/shard_map/ppermute | solution.py:70
  70.8 2.4 %collective-permute-start.5 = (f32[64,16]{0,1:T(8,128)S(1)}, f32[64,16]{0,1:T(8,128)S(1)}, u32[]{:S(2)}, u32[]{:S(2)}) collective-permute-start(f32[64,16]{0,1:T(8,128)S(1)} %slice_add_fusion), channel_id=1, source_target_pairs={{0,2},{1,3},{2,0},{3,1},{4,6},{5,7},{6,4},{7,5},{8,10},{9,11},{10,... | collective-permute-start | bytes 12296 | tf_op jit(solution)/shard_map/ppermute | solution.py:70
  73.2 1.6 %collective-permute-done.5 = f32[64,16]{0,1:T(8,128)S(1)} collective-permute-done((f32[64,16]{0,1:T(8,128)S(1)}, f32[64,16]{0,1:T(8,128)S(1)}, u32[]{:S(2)}, u32[]{:S(2)}) %collective-permute-start.5) | collective-permute-done | bytes 4128 | tf_op jit(solution)/shard_map/ppermute | solution.py:70
  74.8 4.8 %collective-permute-start.6 = (f32[64,16]{0,1:T(8,128)S(1)}, f32[64,16]{0,1:T(8,128)S(1)}, u32[]{:S(2)}, u32[]{:S(2)}) collective-permute-start(f32[64,16]{0,1:T(8,128)S(1)} %add.29), channel_id=1, source_target_pairs={{0,4},{1,5},{2,6},{3,7},{4,0},{5,1},{6,2},{7,3},{8,12},{9,13},{10,... | collective-permute-start | bytes 12296 | tf_op jit(solution)/shard_map/ppermute | solution.py:70
  79.6 1.7 %collective-permute-done.6 = f32[64,16]{0,1:T(8,128)S(1)} collective-permute-done((f32[64,16]{0,1:T(8,128)S(1)}, f32[64,16]{0,1:T(8,128)S(1)}, u32[]{:S(2)}, u32[]{:S(2)}) %collective-permute-start.6) | collective-permute-done | bytes 4128 | tf_op jit(solution)/shard_map/ppermute | solution.py:70
  81.3 2.5 %collective-permute-start.7 = (f32[64,16]{0,1:T(8,128)S(1)}, f32[64,16]{0,1:T(8,128)S(1)}, u32[]{:S(2)}, u32[]{:S(2)}) collective-permute-start(f32[64,16]{0,1:T(8,128)S(1)} %add.30), channel_id=1, source_target_pairs={{0,8},{1,9},{2,10},{3,11},{4,12},{5,13},{6,14},{7,15},{8,0},{9,1},... | collective-permute-start | bytes 12296 | tf_op jit(solution)/shard_map/ppermute | solution.py:70
  83.8 0.7 copy.21
  84.5 4.3 %collective-permute-done.7 = f32[64,16]{0,1:T(8,128)S(1)} collective-permute-done((f32[64,16]{0,1:T(8,128)S(1)}, f32[64,16]{0,1:T(8,128)S(1)}, u32[]{:S(2)}, u32[]{:S(2)}) %collective-permute-start.7) | collective-permute-done | bytes 4128 | tf_op jit(solution)/shard_map/ppermute | solution.py:70
  88.9 0.6 add_multiply_fusion
  89.6 0.6 broadcast_multiply_fusion
  (13 shorter events, 0.2 us)
Async XLA Ops:
  2.2 25.2 %all-to-all-start = ((bf16[16,64,256]{2,1,0:T(8,128)(2,1)}), bf16[16,64,256]{2,1,0:T(8,128)(2,1)S(1)}, u32[]{:S(2)}, u32[]{:S(2)}) async-start(bf16[16,64,256]{2,1,0:T(8,128)(2,1)} %broadcast_in_dim.2), calls=%async_computation | async-start | bytes 1048576 | tf_op jit(solution)/shard_map/all_to_all | solution.py:62
  42.9 46.6 %all-to-all-start.1 = ((f32[16,64,256]{2,1,0:T(8,128)}), f32[16,64,256]{2,1,0:T(8,128)S(1)}, u32[]{:S(2)}, u32[]{:S(2)}) async-start(f32[16,64,256]{2,1,0:T(8,128)} %bitcast.14), calls=%async_computation.1 | async-start | bytes 2097152 | tf_op jit(solution)/shard_map/all_to_all | solution.py:107
  49.9 1.3 %collective-permute-start = (f32[64,80]{0,1:T(8,128)S(1)}, f32[64,80]{0,1:T(8,128)S(1)}, u32[]{:S(2)}, u32[]{:S(2)}) collective-permute-start(f32[64,80]{0,1:T(8,128)S(1)} %pad_maximum_fusion), channel_id=1, source_target_pairs={{0,16},{16,0},{32,48},{48,32},{64,80},{80,64},{96,112},{112,96},{1... | collective-permute-start | bytes 61448 | tf_op jit(solution)/shard_map/ppermute | solution.py:70
  51.2 5.8 %collective-permute-start.1 = (f32[64,80]{0,1:T(8,128)S(1)}, f32[64,80]{0,1:T(8,128)S(1)}, u32[]{:S(2)}, u32[]{:S(2)}) collective-permute-start(f32[64,80]{0,1:T(8,128)S(1)} %fusion), channel_id=1, source_target_pairs={{0,32},{16,48},{32,0},{48,16},{64,96},{80,112},{96,64},{112,80},{1... | collective-permute-start | bytes 61448 | tf_op jit(solution)/shard_map/ppermute | solution.py:70
  57.0 4.0 %collective-permute-start.2 = (f32[64,80]{0,1:T(8,128)S(1)}, f32[64,80]{0,1:T(8,128)S(1)}, u32[]{:S(2)}, u32[]{:S(2)}) collective-permute-start(f32[64,80]{0,1:T(8,128)S(1)} %add.25), channel_id=1, source_target_pairs={{0,64},{16,80},{32,96},{48,112},{64,0},{80,16},{96,32},{112,48},{1... | collective-permute-start | bytes 61448 | tf_op jit(solution)/shard_map/ppermute | solution.py:70
  61.0 5.5 %collective-permute-start.3 = (f32[64,80]{0,1:T(8,128)S(1)}, f32[64,80]{0,1:T(8,128)S(1)}, u32[]{:S(2)}, u32[]{:S(2)}) collective-permute-start(f32[64,80]{0,1:T(8,128)S(1)} %add.26), channel_id=1, source_target_pairs={{0,128},{16,144},{32,160},{48,176},{64,192},{80,208},{96,224},{112... | collective-permute-start | bytes 61448 | tf_op jit(solution)/shard_map/ppermute | solution.py:70
  66.5 4.2 %collective-permute-start.4 = (f32[64,16]{0,1:T(8,128)S(1)}, f32[64,16]{0,1:T(8,128)S(1)}, u32[]{:S(2)}, u32[]{:S(2)}) collective-permute-start(f32[64,16]{0,1:T(8,128)S(1)} %slice.9), channel_id=1, source_target_pairs={{0,1},{1,0},{2,3},{3,2},{4,5},{5,4},{6,7},{7,6},{8,9},{9,8},{10,11... | collective-permute-start | bytes 12296 | tf_op jit(solution)/shard_map/ppermute | solution.py:70
  70.8 4.1 %collective-permute-start.5 = (f32[64,16]{0,1:T(8,128)S(1)}, f32[64,16]{0,1:T(8,128)S(1)}, u32[]{:S(2)}, u32[]{:S(2)}) collective-permute-start(f32[64,16]{0,1:T(8,128)S(1)} %slice_add_fusion), channel_id=1, source_target_pairs={{0,2},{1,3},{2,0},{3,1},{4,6},{5,7},{6,4},{7,5},{8,10},{9,11},{10,... | collective-permute-start | bytes 12296 | tf_op jit(solution)/shard_map/ppermute | solution.py:70
  74.8 6.5 %collective-permute-start.6 = (f32[64,16]{0,1:T(8,128)S(1)}, f32[64,16]{0,1:T(8,128)S(1)}, u32[]{:S(2)}, u32[]{:S(2)}) collective-permute-start(f32[64,16]{0,1:T(8,128)S(1)} %add.29), channel_id=1, source_target_pairs={{0,4},{1,5},{2,6},{3,7},{4,0},{5,1},{6,2},{7,3},{8,12},{9,13},{10,... | collective-permute-start | bytes 12296 | tf_op jit(solution)/shard_map/ppermute | solution.py:70
  81.3 7.6 %collective-permute-start.7 = (f32[64,16]{0,1:T(8,128)S(1)}, f32[64,16]{0,1:T(8,128)S(1)}, u32[]{:S(2)}, u32[]{:S(2)}) collective-permute-start(f32[64,16]{0,1:T(8,128)S(1)} %add.30), channel_id=1, source_target_pairs={{0,8},{1,9},{2,10},{3,11},{4,12},{5,13},{6,14},{7,15},{8,0},{9,1},... | collective-permute-start | bytes 12296 | tf_op jit(solution)/shard_map/ppermute | solution.py:70

commit v4 on v3

--- a/solution.py
+++ b/solution.py
@@ -10,17 +10,23 @@
 ROW_TILE = 512
 
 
-def fused_kernel(obs_ref, factor_t_ref, factor_ref, khatri_ref, node_ref, contracted_ref):
+def fused_kernel(obs_ref, gathered_ref, khatri_ref, node_ref, contracted_ref):
     step = pl.program_id(0)
+    pieces, _, piece = gathered_ref.shape
     khatri = khatri_ref[...]
-    modelled = jnp.dot(factor_t_ref[...], khatri, preferred_element_type=jnp.float32)
+    factor = jnp.concatenate([gathered_ref[c] for c in range(pieces)], axis=1)
+    modelled = lax.dot_general(
+        factor, khatri, (((0,), (0,)), ((), ())), preferred_element_type=jnp.float32
+    )
     derivative = ((modelled - obs_ref[...].astype(jnp.float32)) / (modelled * modelled)).astype(
         jnp.bfloat16
     )
-    node_ref[...] = lax.dot_general(
+    node = lax.dot_general(
         khatri, derivative, (((1,), (1,)), ((), ())), preferred_element_type=jnp.float32
     )
-    part = jnp.dot(factor_ref[...], derivative, preferred_element_type=jnp.float32)
+    for c in range(pieces):
+        node_ref[c] = node[:, c * piece : (c + 1) * piece]
+    part = jnp.dot(factor, derivative, preferred_element_type=jnp.float32)
 
     @pl.when(step == 0)
     def _():
@@ -31,29 +37,29 @@
         contracted_ref[...] += part
 
 
-def fused(observed, factor_t, factor, khatri):
+def fused(observed, gathered, khatri):
     rows, width = observed.shape
-    rank = factor.shape[0]
+    count, rank, piece = gathered.shape
     tile = min(ROW_TILE, rows)
+    pieces = tile // piece
     return pl.pallas_call(
         fused_kernel,
         grid=(rows // tile,),
         in_specs=[
             pl.BlockSpec((tile, width), lambda i: (i, 0)),
-            pl.BlockSpec((tile, rank), lambda i: (i, 0)),
-            pl.BlockSpec((rank, tile), lambda i: (0, i)),
+            pl.BlockSpec((pieces, rank, piece), lambda i: (i, 0, 0)),
             pl.BlockSpec((rank, width), lambda i: (0, 0)),
         ],
         out_specs=[
-            pl.BlockSpec((rank, tile), lambda i: (0, i)),
+            pl.BlockSpec((pieces, rank, piece), lambda i: (i, 0, 0)),
             pl.BlockSpec((rank, width), lambda i: (0, 0)),
         ],
         out_shape=[
-            jax.ShapeDtypeStruct((rank, rows), jnp.float32),
+            jax.ShapeDtypeStruct((count, rank, piece), jnp.float32),
             jax.ShapeDtypeStruct((rank, width), jnp.float32),
         ],
         compiler_params=pltpu.CompilerParams(dimension_semantics=("arbitrary",)),
-    )(observed, factor_t, factor, khatri)
+    )(observed, gathered, khatri)
 
 
 def gather_blocks(values, axis):
@@ -82,7 +88,6 @@
     tm_count = lax.axis_size("tm")
     steps_all = time_dev * tm_count
     nodes_all = node_rows * lax.axis_size("node")
-    share_rows = node_rows // tm_count
 
     khatri = (
         (time_vals[:, :, None] * species_vals[:, None, :])
@@ -90,9 +95,7 @@
         .astype(jnp.bfloat16)
     )
     gathered = gather_blocks(node_factor, "tm")
-    factor = gathered.transpose(1, 0, 2).reshape(factor_rank, node_rows)
-    factor_t = gathered.transpose(0, 2, 1).reshape(node_rows, factor_rank)
-    node_part, contracted_t = fused(observed, factor_t, factor, khatri)
+    blocks, contracted_t = fused(observed, gathered, khatri)
     by_step = contracted_t.reshape(factor_rank, time_dev, species)
     time_part = (by_step * species_vals[:, None, :]).sum(2)
     species_part = (by_step * time_vals[:, :, None]).sum(1)
@@ -103,7 +106,6 @@
     species_sum = butterfly_sum(small_sum[:, time_dev:], "tm")
     grad_species = species_sum / math.sqrt(nodes_all * steps_all)
 
-    blocks = node_part.reshape(factor_rank, tm_count, share_rows).transpose(1, 0, 2)
     summed = lax.all_to_all(blocks, "tm", 0, 0, tiled=True).sum(0)
     grad_node = summed / math.sqrt(steps_all * species)
     return (grad_node, grad_time, grad_species)

time: 90.9 us -> 87.5 us (0.963)
  local copies, waits for them, and re-layouts: 9.57 us -> 5.84 us
    reshape x2 -> x0, local copies, waits for them, and re-layouts: 3.19 us -> none  [the longest x1 2.36 us: shards(): node_part.reshape(factor_rank, tm_count, share_rows).transpose(1, 0, 2)]
    transpose x1 -> x0, local copies, waits for them, and re-layouts: 1.37 us -> none  [shards(): factor_t = gathered.transpose(0, 2, 1).reshape(node_rows, factor_rank)]
where the time goes in v4:
time: 87.5 us; the launch traced here: 86.9 us
  waiting for transfers between devices  38 us (43%)
  starting transfers between devices  28.7 us (33%)
  Pallas kernels  11.4 us (13%)
  local copies, waits for them, and re-layouts  5.84 us (7%)
  other arithmetic  2.27 us (3%)
    ppermute x8, waiting for transfers between devices, butterfly_sum(): values = values + lax.ppermute(values, axis, pairs)  25.1 us
    ppermute x8, starting transfers between devices, butterfly_sum(): values = values + lax.ppermute(values, axis, pairs)  13.2 us
    all_to_all x1, waiting for transfers between devices, gather_blocks(): return lax.all_to_all(copies, axis, 0, 0, tiled=True)  12.9 us
    pallas_call x1, Pallas kernels, fused(): pl.pallas_call(fused_kernel, grid=(rows // tile,), in_specs=[pl.BlockSpec...  11.4 us
    all_to_all x1, starting transfers between devices, gather_blocks(): return lax.all_to_all(copies, axis, 0, 0, tiled=True)  9.94 us
    all_to_all x1, starting transfers between devices, shards(): summed = lax.all_to_all(blocks, 'tm', 0, 0, tiled=True).sum(0)  5.6 us
  transfers between devices with their start and end apart: 10, of which 9 were waited for; matrix products, arithmetic and copies ran while one was open for 6% of the time, Pallas kernels for 0%

profile of v4, /device:TPU:22, one launch (start us, length us, event | category | flops | bytes accessed | tf_op | source)
XLA Modules:
  0.0 86.9 jit_solution(1111315746686167236)
XLA Ops:
  0.6 1.6 %broadcast_in_dim.2 = bf16[16,64,256]{2,1,0:T(8,128)(2,1)} broadcast(bf16[64,256]{1,0:T(8,128)(2,1)} %param.5), dimensions={1,2} | broadcast | bytes 557056 | tf_op jit(solution)/shard_map/broadcast_in_dim | solution.py:67
  2.2 9.9 %all-to-all-start = ((bf16[16,64,256]{2,1,0:T(8,128)(2,1)}), bf16[16,64,256]{2,1,0:T(8,128)(2,1)S(1)}, u32[]{:S(2)}, u32[]{:S(2)}) async-start(bf16[16,64,256]{2,1,0:T(8,128)(2,1)} %broadcast_in_dim.2), calls=%async_computation | async-start | bytes 1048576 | tf_op jit(solution)/shard_map/all_to_all | solution.py:68
  12.2 0.8 copy.9
  13.0 0.7 convert_element_type.12
  13.7 0.1 multiply_convert_fusion
  13.7 0.8 copy.10.khatri_ref
  14.5 12.9 %all-to-all-done.gathered_ref = bf16[16,64,256]{2,1,0:T(8,128)(2,1)S(1)} async-done(((bf16[16,64,256]{2,1,0:T(8,128)(2,1)}), bf16[16,64,256]{2,1,0:T(8,128)(2,1)S(1)}, u32[]{:S(2)}, u32[]{:S(2)}) %all-to-all-start) | async-done | bytes 524320 | tf_op jit(solution)/shard_map/all_to_all | solution.py:68
  27.4 0.8 copy-done
  28.2 11.4 %shard_map.67 = (f32[16,64,256]{2,1,0:T(8,128)}, f32[64,1024]{1,0:T(8,128)}) custom-call(bf16[4096,1024]{1,0:T(8,128)(2,1)} %obs_ref.1, bf16[16,64,256]{2,1,0:T(8,128)(2,1)} %copy-done, bf16[64,1024]{1,0:T(8,128)(2,1)} %copy.10.khatri_ref), custom_call_target="tpu_custom_call" | custom-call | tf_op jit(solution)/shard_map/pallas_call | solution.py:45
  39.6 5.6 %all-to-all-start.1 = ((f32[16,64,256]{2,1,0:T(8,128)}), f32[16,64,256]{2,1,0:T(8,128)S(1)}, u32[]{:S(2)}, u32[]{:S(2)}) async-start(f32[16,64,256]{2,1,0:T(8,128)} %get-tuple-element.5), calls=%async_computation.1 | async-start | bytes 2097152 | tf_op jit(solution)/shard_map/all_to_all | solution.py:109
  45.2 1.1 %copy.11 = f32[64,1024]{0,1:T(8,128)S(1)} copy(f32[64,1024]{1,0:T(8,128)} %get-tuple-element.6) | data formatting | bytes 524288 | tf_op jit(solution)/shard_map/pallas_call | solution.py:45
  46.4 0.2 multiply_reduce_fusion
  46.5 0.1 collective-permute-start
  46.6 1.2 %collective-permute-done = f32[64,80]{0,1:T(8,128)S(1)} collective-permute-done((f32[64,80]{0,1:T(8,128)S(1)}, f32[64,80]{0,1:T(8,128)S(1)}, u32[]{:S(2)}, u32[]{:S(2)}) %collective-permute-start) | collective-permute-done | bytes 20512 | tf_op jit(solution)/shard_map/ppermute | solution.py:76
  47.9 1.5 %collective-permute-start.1 = (f32[64,80]{0,1:T(8,128)S(1)}, f32[64,80]{0,1:T(8,128)S(1)}, u32[]{:S(2)}, u32[]{:S(2)}) collective-permute-start(f32[64,80]{0,1:T(8,128)S(1)} %fusion), channel_id=1, source_target_pairs={{0,32},{16,48},{32,0},{48,16},{64,96},{80,112},{96,64},{112,80},{1... | collective-permute-start | bytes 61448 | tf_op jit(solution)/shard_map/ppermute | solution.py:76
  49.4 4.3 %collective-permute-done.1 = f32[64,80]{0,1:T(8,128)S(1)} collective-permute-done((f32[64,80]{0,1:T(8,128)S(1)}, f32[64,80]{0,1:T(8,128)S(1)}, u32[]{:S(2)}, u32[]{:S(2)}) %collective-permute-start.1) | collective-permute-done | bytes 20512 | tf_op jit(solution)/shard_map/ppermute | solution.py:76
  53.7 1.3 %collective-permute-start.2 = (f32[64,80]{0,1:T(8,128)S(1)}, f32[64,80]{0,1:T(8,128)S(1)}, u32[]{:S(2)}, u32[]{:S(2)}) collective-permute-start(f32[64,80]{0,1:T(8,128)S(1)} %add.25), channel_id=1, source_target_pairs={{0,64},{16,80},{32,96},{48,112},{64,0},{80,16},{96,32},{112,48},{1... | collective-permute-start | bytes 61448 | tf_op jit(solution)/shard_map/ppermute | solution.py:76
  55.0 2.7 %collective-permute-done.2 = f32[64,80]{0,1:T(8,128)S(1)} collective-permute-done((f32[64,80]{0,1:T(8,128)S(1)}, f32[64,80]{0,1:T(8,128)S(1)}, u32[]{:S(2)}, u32[]{:S(2)}) %collective-permute-start.2) | collective-permute-done | bytes 20512 | tf_op jit(solution)/shard_map/ppermute | solution.py:76
  57.7 0.3 collective-permute-start.3
  58.0 5.2 %collective-permute-done.3 = f32[64,80]{0,1:T(8,128)S(1)} collective-permute-done((f32[64,80]{0,1:T(8,128)S(1)}, f32[64,80]{0,1:T(8,128)S(1)}, u32[]{:S(2)}, u32[]{:S(2)}) %collective-permute-start.3) | collective-permute-done | bytes 20512 | tf_op jit(solution)/shard_map/ppermute | solution.py:76
  63.2 0.2 collective-permute-start.4
  63.4 4.0 %collective-permute-done.4 = f32[64,16]{0,1:T(8,128)S(1)} collective-permute-done((f32[64,16]{0,1:T(8,128)S(1)}, f32[64,16]{0,1:T(8,128)S(1)}, u32[]{:S(2)}, u32[]{:S(2)}) %collective-permute-start.4) | collective-permute-done | bytes 4128 | tf_op jit(solution)/shard_map/ppermute | solution.py:76
  67.4 2.4 %collective-permute-start.5 = (f32[64,16]{0,1:T(8,128)S(1)}, f32[64,16]{0,1:T(8,128)S(1)}, u32[]{:S(2)}, u32[]{:S(2)}) collective-permute-start(f32[64,16]{0,1:T(8,128)S(1)} %slice_add_fusion), channel_id=1, source_target_pairs={{0,2},{1,3},{2,0},{3,1},{4,6},{5,7},{6,4},{7,5},{8,10},{9,11},{10,... | collective-permute-start | bytes 12296 | tf_op jit(solution)/shard_map/ppermute | solution.py:76
  69.9 1.6 %collective-permute-done.5 = f32[64,16]{0,1:T(8,128)S(1)} collective-permute-done((f32[64,16]{0,1:T(8,128)S(1)}, f32[64,16]{0,1:T(8,128)S(1)}, u32[]{:S(2)}, u32[]{:S(2)}) %collective-permute-start.5) | collective-permute-done | bytes 4128 | tf_op jit(solution)/shard_map/ppermute | solution.py:76
  71.5 4.8 %collective-permute-start.6 = (f32[64,16]{0,1:T(8,128)S(1)}, f32[64,16]{0,1:T(8,128)S(1)}, u32[]{:S(2)}, u32[]{:S(2)}) collective-permute-start(f32[64,16]{0,1:T(8,128)S(1)} %add.29), channel_id=1, source_target_pairs={{0,4},{1,5},{2,6},{3,7},{4,0},{5,1},{6,2},{7,3},{8,12},{9,13},{10,... | collective-permute-start | bytes 12296 | tf_op jit(solution)/shard_map/ppermute | solution.py:76
  76.3 1.7 %collective-permute-done.6 = f32[64,16]{0,1:T(8,128)S(1)} collective-permute-done((f32[64,16]{0,1:T(8,128)S(1)}, f32[64,16]{0,1:T(8,128)S(1)}, u32[]{:S(2)}, u32[]{:S(2)}) %collective-permute-start.6) | collective-permute-done | bytes 4128 | tf_op jit(solution)/shard_map/ppermute | solution.py:76
  78.0 2.5 %collective-permute-start.7 = (f32[64,16]{0,1:T(8,128)S(1)}, f32[64,16]{0,1:T(8,128)S(1)}, u32[]{:S(2)}, u32[]{:S(2)}) collective-permute-start(f32[64,16]{0,1:T(8,128)S(1)} %add.30), channel_id=1, source_target_pairs={{0,8},{1,9},{2,10},{3,11},{4,12},{5,13},{6,14},{7,15},{8,0},{9,1},... | collective-permute-start | bytes 12296 | tf_op jit(solution)/shard_map/ppermute | solution.py:76
  80.5 0.7 copy.12
  81.2 4.3 %collective-permute-done.7 = f32[64,16]{0,1:T(8,128)S(1)} collective-permute-done((f32[64,16]{0,1:T(8,128)S(1)}, f32[64,16]{0,1:T(8,128)S(1)}, u32[]{:S(2)}, u32[]{:S(2)}) %collective-permute-start.7) | collective-permute-done | bytes 4128 | tf_op jit(solution)/shard_map/ppermute | solution.py:76
  85.6 0.6 add_multiply_fusion
  86.2 0.1 reduce_sum.27
  86.2 0.6 broadcast_multiply_fusion
  (12 shorter events, 0.1 us)
Async XLA Ops:
  2.2 25.2 %all-to-all-start = ((bf16[16,64,256]{2,1,0:T(8,128)(2,1)}), bf16[16,64,256]{2,1,0:T(8,128)(2,1)S(1)}, u32[]{:S(2)}, u32[]{:S(2)}) async-start(bf16[16,64,256]{2,1,0:T(8,128)(2,1)} %broadcast_in_dim.2), calls=%async_computation | async-start | bytes 1048576 | tf_op jit(solution)/shard_map/all_to_all | solution.py:68
  27.4 0.8 copy-start
  39.6 46.6 %all-to-all-start.1 = ((f32[16,64,256]{2,1,0:T(8,128)}), f32[16,64,256]{2,1,0:T(8,128)S(1)}, u32[]{:S(2)}, u32[]{:S(2)}) async-start(f32[16,64,256]{2,1,0:T(8,128)} %get-tuple-element.5), calls=%async_computation.1 | async-start | bytes 2097152 | tf_op jit(solution)/shard_map/all_to_all | solution.py:109
  46.5 1.3 %collective-permute-start = (f32[64,80]{0,1:T(8,128)S(1)}, f32[64,80]{0,1:T(8,128)S(1)}, u32[]{:S(2)}, u32[]{:S(2)}) collective-permute-start(f32[64,80]{0,1:T(8,128)S(1)} %pad_maximum_fusion), channel_id=1, source_target_pairs={{0,16},{16,0},{32,48},{48,32},{64,80},{80,64},{96,112},{112,96},{1... | collective-permute-start | bytes 61448 | tf_op jit(solution)/shard_map/ppermute | solution.py:76
  47.9 5.8 %collective-permute-start.1 = (f32[64,80]{0,1:T(8,128)S(1)}, f32[64,80]{0,1:T(8,128)S(1)}, u32[]{:S(2)}, u32[]{:S(2)}) collective-permute-start(f32[64,80]{0,1:T(8,128)S(1)} %fusion), channel_id=1, source_target_pairs={{0,32},{16,48},{32,0},{48,16},{64,96},{80,112},{96,64},{112,80},{1... | collective-permute-start | bytes 61448 | tf_op jit(solution)/shard_map/ppermute | solution.py:76
  53.7 4.0 %collective-permute-start.2 = (f32[64,80]{0,1:T(8,128)S(1)}, f32[64,80]{0,1:T(8,128)S(1)}, u32[]{:S(2)}, u32[]{:S(2)}) collective-permute-start(f32[64,80]{0,1:T(8,128)S(1)} %add.25), channel_id=1, source_target_pairs={{0,64},{16,80},{32,96},{48,112},{64,0},{80,16},{96,32},{112,48},{1... | collective-permute-start | bytes 61448 | tf_op jit(solution)/shard_map/ppermute | solution.py:76
  57.7 5.5 %collective-permute-start.3 = (f32[64,80]{0,1:T(8,128)S(1)}, f32[64,80]{0,1:T(8,128)S(1)}, u32[]{:S(2)}, u32[]{:S(2)}) collective-permute-start(f32[64,80]{0,1:T(8,128)S(1)} %add.26), channel_id=1, source_target_pairs={{0,128},{16,144},{32,160},{48,176},{64,192},{80,208},{96,224},{112... | collective-permute-start | bytes 61448 | tf_op jit(solution)/shard_map/ppermute | solution.py:76
  63.2 4.2 %collective-permute-start.4 = (f32[64,16]{0,1:T(8,128)S(1)}, f32[64,16]{0,1:T(8,128)S(1)}, u32[]{:S(2)}, u32[]{:S(2)}) collective-permute-start(f32[64,16]{0,1:T(8,128)S(1)} %slice.9), channel_id=1, source_target_pairs={{0,1},{1,0},{2,3},{3,2},{4,5},{5,4},{6,7},{7,6},{8,9},{9,8},{10,11... | collective-permute-start | bytes 12296 | tf_op jit(solution)/shard_map/ppermute | solution.py:76
  67.4 4.1 %collective-permute-start.5 = (f32[64,16]{0,1:T(8,128)S(1)}, f32[64,16]{0,1:T(8,128)S(1)}, u32[]{:S(2)}, u32[]{:S(2)}) collective-permute-start(f32[64,16]{0,1:T(8,128)S(1)} %slice_add_fusion), channel_id=1, source_target_pairs={{0,2},{1,3},{2,0},{3,1},{4,6},{5,7},{6,4},{7,5},{8,10},{9,11},{10,... | collective-permute-start | bytes 12296 | tf_op jit(solution)/shard_map/ppermute | solution.py:76
  71.5 6.5 %collective-permute-start.6 = (f32[64,16]{0,1:T(8,128)S(1)}, f32[64,16]{0,1:T(8,128)S(1)}, u32[]{:S(2)}, u32[]{:S(2)}) collective-permute-start(f32[64,16]{0,1:T(8,128)S(1)} %add.29), channel_id=1, source_target_pairs={{0,4},{1,5},{2,6},{3,7},{4,0},{5,1},{6,2},{7,3},{8,12},{9,13},{10,... | collective-permute-start | bytes 12296 | tf_op jit(solution)/shard_map/ppermute | solution.py:76
  78.0 7.6 %collective-permute-start.7 = (f32[64,16]{0,1:T(8,128)S(1)}, f32[64,16]{0,1:T(8,128)S(1)}, u32[]{:S(2)}, u32[]{:S(2)}) collective-permute-start(f32[64,16]{0,1:T(8,128)S(1)} %add.30), channel_id=1, source_target_pairs={{0,8},{1,9},{2,10},{3,11},{4,12},{5,13},{6,14},{7,15},{8,0},{9,1},... | collective-permute-start | bytes 12296 | tf_op jit(solution)/shard_map/ppermute | solution.py:76

commit v5 on v4

--- a/solution.py
+++ b/solution.py
@@ -26,7 +26,9 @@
     )
     for c in range(pieces):
         node_ref[c] = node[:, c * piece : (c + 1) * piece]
-    part = jnp.dot(factor, derivative, preferred_element_type=jnp.float32)
+    part = lax.dot_general(
+        derivative, factor, (((0,), (1,)), ((), ())), preferred_element_type=jnp.float32
+    )
 
     @pl.when(step == 0)
     def _():
@@ -52,11 +54,11 @@
         ],
         out_specs=[
             pl.BlockSpec((pieces, rank, piece), lambda i: (i, 0, 0)),
-            pl.BlockSpec((rank, width), lambda i: (0, 0)),
+            pl.BlockSpec((width, rank), lambda i: (0, 0)),
         ],
         out_shape=[
             jax.ShapeDtypeStruct((count, rank, piece), jnp.float32),
-            jax.ShapeDtypeStruct((rank, width), jnp.float32),
+            jax.ShapeDtypeStruct((width, rank), jnp.float32),
         ],
         compiler_params=pltpu.CompilerParams(dimension_semantics=("arbitrary",)),
     )(observed, gathered, khatri)
@@ -95,10 +97,10 @@
         .astype(jnp.bfloat16)
     )
     gathered = gather_blocks(node_factor, "tm")
-    blocks, contracted_t = fused(observed, gathered, khatri)
-    by_step = contracted_t.reshape(factor_rank, time_dev, species)
-    time_part = (by_step * species_vals[:, None, :]).sum(2)
-    species_part = (by_step * time_vals[:, :, None]).sum(1)
+    blocks, contracted = fused(observed, gathered, khatri)
+    by_step = contracted.reshape(time_dev, species, factor_rank)
+    time_part = (by_step * species_vals.T[None, :, :]).sum(1).T
+    species_part = (by_step * time_vals.T[:, None, :]).sum(0).T
 
     small = jnp.concatenate([time_part, species_part], axis=1)
     small_sum = butterfly_sum(small, "node")

time: 87.5 us -> 88.9 us (1.016)
  starting transfers between devices: 28.7 us -> 23.1 us
  waiting for transfers between devices: 38 us -> 43.1 us
  other arithmetic: 2.27 us -> 4.4 us
  local copies, waits for them, and re-layouts: 5.84 us -> 4.77 us
    ppermute x8, starting transfers between devices: 13.2 us -> 7.54 us  [butterfly_sum(): values = values + lax.ppermute(values, axis, pairs)]
    ppermute x8, waiting for transfers between devices: 25.1 us -> 30.2 us  [butterfly_sum(): values = values + lax.ppermute(values, axis, pairs)]
    reduce_sum x1 -> x2, other arithmetic: 0.17 us -> 2.3 us  [the longest x1 1.16 us: shards(): time_part = (by_step * species_vals.T[None, :, :]).sum(1).T]
    pallas_call x1 -> x0, local copies, waits for them, and re-layouts: 1.14 us -> none  [fused(): pl.pallas_call(fused_kernel, grid=(rows // tile,), in_specs=[pl.BlockSpec...]
  transfers between devices with their start and end apart: 10 -> 10, of which waited for: 9 -> 9; matrix products, arithmetic and copies ran while one was open for 6% -> 7% of each run, Pallas kernels for 0% -> 0%
where the time goes in v5:
time: 88.9 us; the launch traced here: 88.1 us
  waiting for transfers between devices  43.1 us (48%)
  starting transfers between devices  23.1 us (26%)
  Pallas kernels  12.1 us (14%)
  local copies, waits for them, and re-layouts  4.77 us (5%)
  other arithmetic  4.4 us (5%)
    ppermute x8, waiting for transfers between devices, butterfly_sum(): values = values + lax.ppermute(values, axis, pairs)  30.2 us
    all_to_all x1, waiting for transfers between devices, gather_blocks(): return lax.all_to_all(copies, axis, 0, 0, tiled=True)  12.9 us
    pallas_call x1, Pallas kernels, fused(): pl.pallas_call(fused_kernel, grid=(rows // tile,), in_specs=[pl.BlockSpec...  12.1 us
    all_to_all x1, starting transfers between devices, gather_blocks(): return lax.all_to_all(copies, axis, 0, 0, tiled=True)  9.94 us
    ppermute x8, starting transfers between devices, butterfly_sum(): values = values + lax.ppermute(values, axis, pairs)  7.54 us
    all_to_all x1, starting transfers between devices, shards(): summed = lax.all_to_all(blocks, 'tm', 0, 0, tiled=True).sum(0)  5.6 us
  transfers between devices with their start and end apart: 10, of which 9 were waited for; matrix products, arithmetic and copies ran while one was open for 7% of the time, Pallas kernels for 0%

profile of v5, /device:TPU:22, one launch (start us, length us, event | category | flops | bytes accessed | tf_op | source)
XLA Modules:
  0.0 88.1 jit_solution(16489582521602221367)
XLA Ops:
  0.6 0.0 copy-start.1
  0.6 1.6 %broadcast_in_dim.2 = bf16[16,64,256]{2,1,0:T(8,128)(2,1)} broadcast(bf16[64,256]{1,0:T(8,128)(2,1)} %param.5), dimensions={1,2} | broadcast | bytes 557056 | tf_op jit(solution)/shard_map/broadcast_in_dim | solution.py:69
  2.2 9.9 %all-to-all-start = ((bf16[16,64,256]{2,1,0:T(8,128)(2,1)}), bf16[16,64,256]{2,1,0:T(8,128)(2,1)S(1)}, u32[]{:S(2)}, u32[]{:S(2)}) async-start(bf16[16,64,256]{2,1,0:T(8,128)(2,1)} %broadcast_in_dim.2), calls=%async_computation | async-start | bytes 1048576 | tf_op jit(solution)/shard_map/all_to_all | solution.py:70
  12.2 0.8 copy.10
  13.0 0.7 convert_bitcast_fusion.1
  13.7 0.8 copy.11.khatri_ref
  14.5 12.9 %all-to-all-done.gathered_ref = bf16[16,64,256]{2,1,0:T(8,128)(2,1)S(1)} async-done(((bf16[16,64,256]{2,1,0:T(8,128)(2,1)}), bf16[16,64,256]{2,1,0:T(8,128)(2,1)S(1)}, u32[]{:S(2)}, u32[]{:S(2)}) %all-to-all-start) | async-done | bytes 524320 | tf_op jit(solution)/shard_map/all_to_all | solution.py:70
  27.4 0.8 copy-done
  28.2 12.1 %shard_map.67 = (f32[16,64,256]{2,1,0:T(8,128)}, f32[1024,64]{1,0:T(8,128)}) custom-call(bf16[4096,1024]{1,0:T(8,128)(2,1)} %obs_ref.1, bf16[16,64,256]{2,1,0:T(8,128)(2,1)} %copy-done, bf16[64,1024]{1,0:T(8,128)(2,1)} %copy.11.khatri_ref), custom_call_target="tpu_custom_call" | custom-call | tf_op jit(solution)/shard_map/pallas_call | solution.py:47
  40.3 5.6 %all-to-all-start.1 = ((f32[16,64,256]{2,1,0:T(8,128)}), f32[16,64,256]{2,1,0:T(8,128)S(1)}, u32[]{:S(2)}, u32[]{:S(2)}) async-start(f32[16,64,256]{2,1,0:T(8,128)} %get-tuple-element.5), calls=%async_computation.1 | async-start | bytes 2097152 | tf_op jit(solution)/shard_map/all_to_all | solution.py:111
  45.9 0.1 copy.12
  46.0 1.2 %multiply_reduce_fusion.1 = f32[64,64]{1,0:T(8,128)S(1)} fusion(f32[16,64]{1,0:T(8,128)S(1)} %get-tuple-element.13, f32[1024,64]{1,0:T(8,128)} %get-tuple-element.6), kind=kLoop, calls=%fused_computation.1 | loop fusion | flops 126976 | bytes 282624 | tf_op jit(solution)/shard_map/reduce_sum | solution.py:102
  47.2 1.1 %multiply_reduce_fusion = f32[16,64]{1,0:T(8,128)S(1)} fusion(f32[64,16,64]{2,1,0:T(8,128)} %bitcast.9, f32[64,64]{1,0:T(8,128)S(1)} %copy.12), kind=kLoop, calls=%fused_computation | loop fusion | flops 130048 | bytes 282624 | tf_op jit(solution)/shard_map/reduce_sum | solution.py:103
  48.3 0.1 collective-permute-start
  48.4 1.2 %collective-permute-done = f32[64,80]{0,1:T(8,128)S(1)} collective-permute-done((f32[64,80]{0,1:T(8,128)S(1)}, f32[64,80]{0,1:T(8,128)S(1)}, u32[]{:S(2)}, u32[]{:S(2)}) %collective-permute-start) | collective-permute-done | bytes 20512 | tf_op jit(solution)/shard_map/ppermute | solution.py:78
  49.6 1.5 %collective-permute-start.1 = (f32[64,80]{0,1:T(8,128)S(1)}, f32[64,80]{0,1:T(8,128)S(1)}, u32[]{:S(2)}, u32[]{:S(2)}) collective-permute-start(f32[64,80]{0,1:T(8,128)S(1)} %fusion), channel_id=1, source_target_pairs={{0,32},{16,48},{32,0},{48,16},{64,96},{80,112},{96,64},{112,80},{1... | collective-permute-start | bytes 61448 | tf_op jit(solution)/shard_map/ppermute | solution.py:78
  51.1 4.2 %collective-permute-done.1 = f32[64,80]{0,1:T(8,128)S(1)} collective-permute-done((f32[64,80]{0,1:T(8,128)S(1)}, f32[64,80]{0,1:T(8,128)S(1)}, u32[]{:S(2)}, u32[]{:S(2)}) %collective-permute-start.1) | collective-permute-done | bytes 20512 | tf_op jit(solution)/shard_map/ppermute | solution.py:78
  55.3 1.3 %collective-permute-start.2 = (f32[64,80]{0,1:T(8,128)S(1)}, f32[64,80]{0,1:T(8,128)S(1)}, u32[]{:S(2)}, u32[]{:S(2)}) collective-permute-start(f32[64,80]{0,1:T(8,128)S(1)} %add.25), channel_id=1, source_target_pairs={{0,64},{16,80},{32,96},{48,112},{64,0},{80,16},{96,32},{112,48},{1... | collective-permute-start | bytes 61448 | tf_op jit(solution)/shard_map/ppermute | solution.py:78
  56.6 2.7 %collective-permute-done.2 = f32[64,80]{0,1:T(8,128)S(1)} collective-permute-done((f32[64,80]{0,1:T(8,128)S(1)}, f32[64,80]{0,1:T(8,128)S(1)}, u32[]{:S(2)}, u32[]{:S(2)}) %collective-permute-start.2) | collective-permute-done | bytes 20512 | tf_op jit(solution)/shard_map/ppermute | solution.py:78
  59.3 0.3 collective-permute-start.3
  59.7 5.2 %collective-permute-done.3 = f32[64,80]{0,1:T(8,128)S(1)} collective-permute-done((f32[64,80]{0,1:T(8,128)S(1)}, f32[64,80]{0,1:T(8,128)S(1)}, u32[]{:S(2)}, u32[]{:S(2)}) %collective-permute-start.3) | collective-permute-done | bytes 20512 | tf_op jit(solution)/shard_map/ppermute | solution.py:78
  64.9 0.3 collective-permute-start.4
  65.2 5.8 %collective-permute-done.4 = f32[64,16]{0,1:T(8,128)S(1)} collective-permute-done((f32[64,16]{0,1:T(8,128)S(1)}, f32[64,16]{0,1:T(8,128)S(1)}, u32[]{:S(2)}, u32[]{:S(2)}) %collective-permute-start.4) | collective-permute-done | bytes 4128 | tf_op jit(solution)/shard_map/ppermute | solution.py:78
  71.0 3.6 %collective-permute-done.5 = f32[64,16]{0,1:T(8,128)S(1)} collective-permute-done((f32[64,16]{0,1:T(8,128)S(1)}, f32[64,16]{0,1:T(8,128)S(1)}, u32[]{:S(2)}, u32[]{:S(2)}) %collective-permute-start.5) | collective-permute-done | bytes 4128 | tf_op jit(solution)/shard_map/ppermute | solution.py:78
  74.7 0.8 collective-permute-start.6
  75.5 3.7 %collective-permute-done.6 = f32[64,16]{0,1:T(8,128)S(1)} collective-permute-done((f32[64,16]{0,1:T(8,128)S(1)}, f32[64,16]{0,1:T(8,128)S(1)}, u32[]{:S(2)}, u32[]{:S(2)}) %collective-permute-start.6) | collective-permute-done | bytes 4128 | tf_op jit(solution)/shard_map/ppermute | solution.py:78
  79.2 3.2 %collective-permute-start.7 = (f32[64,16]{0,1:T(8,128)S(1)}, f32[64,16]{0,1:T(8,128)S(1)}, u32[]{:S(2)}, u32[]{:S(2)}) collective-permute-start(f32[64,16]{0,1:T(8,128)S(1)} %add.30), channel_id=1, source_target_pairs={{0,8},{1,9},{2,10},{3,11},{4,12},{5,13},{6,14},{7,15},{8,0},{9,1},... | collective-permute-start | bytes 12296 | tf_op jit(solution)/shard_map/ppermute | solution.py:78
  82.4 0.7 copy.13
  83.1 3.7 %collective-permute-done.7 = f32[64,16]{0,1:T(8,128)S(1)} collective-permute-done((f32[64,16]{0,1:T(8,128)S(1)}, f32[64,16]{0,1:T(8,128)S(1)}, u32[]{:S(2)}, u32[]{:S(2)}) %collective-permute-start.7) | collective-permute-done | bytes 4128 | tf_op jit(solution)/shard_map/ppermute | solution.py:78
  86.8 0.6 add_multiply_fusion
  87.4 0.1 reduce_sum.27
  87.5 0.6 broadcast_multiply_fusion
  (16 shorter events, 0.1 us)
Async XLA Ops:
  0.6 45.3 %copy-start.1 = (bf16[64,64]{1,0:T(8,128)(2,1)S(1)}, bf16[64,64]{1,0:T(8,128)(2,1)}, u32[]{:S(2)}) copy-start(bf16[64,64]{1,0:T(8,128)(2,1)} %param.6) | copy-start | bytes 24580
  2.2 25.2 %all-to-all-start = ((bf16[16,64,256]{2,1,0:T(8,128)(2,1)}), bf16[16,64,256]{2,1,0:T(8,128)(2,1)S(1)}, u32[]{:S(2)}, u32[]{:S(2)}) async-start(bf16[16,64,256]{2,1,0:T(8,128)(2,1)} %broadcast_in_dim.2), calls=%async_computation | async-start | bytes 1048576 | tf_op jit(solution)/shard_map/all_to_all | solution.py:70
  27.4 0.8 copy-start
  40.3 47.1 %all-to-all-start.1 = ((f32[16,64,256]{2,1,0:T(8,128)}), f32[16,64,256]{2,1,0:T(8,128)S(1)}, u32[]{:S(2)}, u32[]{:S(2)}) async-start(f32[16,64,256]{2,1,0:T(8,128)} %get-tuple-element.5), calls=%async_computation.1 | async-start | bytes 2097152 | tf_op jit(solution)/shard_map/all_to_all | solution.py:111
  48.3 1.3 %collective-permute-start = (f32[64,80]{0,1:T(8,128)S(1)}, f32[64,80]{0,1:T(8,128)S(1)}, u32[]{:S(2)}, u32[]{:S(2)}) collective-permute-start(f32[64,80]{0,1:T(8,128)S(1)} %pad_maximum_fusion), channel_id=1, source_target_pairs={{0,16},{16,0},{32,48},{48,32},{64,80},{80,64},{96,112},{112,96},{1... | collective-permute-start | bytes 61448 | tf_op jit(solution)/shard_map/ppermute | solution.py:78
  49.6 5.7 %collective-permute-start.1 = (f32[64,80]{0,1:T(8,128)S(1)}, f32[64,80]{0,1:T(8,128)S(1)}, u32[]{:S(2)}, u32[]{:S(2)}) collective-permute-start(f32[64,80]{0,1:T(8,128)S(1)} %fusion), channel_id=1, source_target_pairs={{0,32},{16,48},{32,0},{48,16},{64,96},{80,112},{96,64},{112,80},{1... | collective-permute-start | bytes 61448 | tf_op jit(solution)/shard_map/ppermute | solution.py:78
  55.3 4.0 %collective-permute-start.2 = (f32[64,80]{0,1:T(8,128)S(1)}, f32[64,80]{0,1:T(8,128)S(1)}, u32[]{:S(2)}, u32[]{:S(2)}) collective-permute-start(f32[64,80]{0,1:T(8,128)S(1)} %add.25), channel_id=1, source_target_pairs={{0,64},{16,80},{32,96},{48,112},{64,0},{80,16},{96,32},{112,48},{1... | collective-permute-start | bytes 61448 | tf_op jit(solution)/shard_map/ppermute | solution.py:78
  59.3 5.5 %collective-permute-start.3 = (f32[64,80]{0,1:T(8,128)S(1)}, f32[64,80]{0,1:T(8,128)S(1)}, u32[]{:S(2)}, u32[]{:S(2)}) collective-permute-start(f32[64,80]{0,1:T(8,128)S(1)} %add.26), channel_id=1, source_target_pairs={{0,128},{16,144},{32,160},{48,176},{64,192},{80,208},{96,224},{112... | collective-permute-start | bytes 61448 | tf_op jit(solution)/shard_map/ppermute | solution.py:78
  64.9 6.1 %collective-permute-start.4 = (f32[64,16]{0,1:T(8,128)S(1)}, f32[64,16]{0,1:T(8,128)S(1)}, u32[]{:S(2)}, u32[]{:S(2)}) collective-permute-start(f32[64,16]{0,1:T(8,128)S(1)} %slice.9), channel_id=1, source_target_pairs={{0,1},{1,0},{2,3},{3,2},{4,5},{5,4},{6,7},{7,6},{8,9},{9,8},{10,11... | collective-permute-start | bytes 12296 | tf_op jit(solution)/shard_map/ppermute | solution.py:78
  71.0 3.7 %collective-permute-start.5 = (f32[64,16]{0,1:T(8,128)S(1)}, f32[64,16]{0,1:T(8,128)S(1)}, u32[]{:S(2)}, u32[]{:S(2)}) collective-permute-start(f32[64,16]{0,1:T(8,128)S(1)} %slice_add_fusion), channel_id=1, source_target_pairs={{0,2},{1,3},{2,0},{3,1},{4,6},{5,7},{6,4},{7,5},{8,10},{9,11},{10,... | collective-permute-start | bytes 12296 | tf_op jit(solution)/shard_map/ppermute | solution.py:78
  74.7 4.6 %collective-permute-start.6 = (f32[64,16]{0,1:T(8,128)S(1)}, f32[64,16]{0,1:T(8,128)S(1)}, u32[]{:S(2)}, u32[]{:S(2)}) collective-permute-start(f32[64,16]{0,1:T(8,128)S(1)} %add.29), channel_id=1, source_target_pairs={{0,4},{1,5},{2,6},{3,7},{4,0},{5,1},{6,2},{7,3},{8,12},{9,13},{10,... | collective-permute-start | bytes 12296 | tf_op jit(solution)/shard_map/ppermute | solution.py:78
  79.2 7.6 %collective-permute-start.7 = (f32[64,16]{0,1:T(8,128)S(1)}, f32[64,16]{0,1:T(8,128)S(1)}, u32[]{:S(2)}, u32[]{:S(2)}) collective-permute-start(f32[64,16]{0,1:T(8,128)S(1)} %add.30), channel_id=1, source_target_pairs={{0,8},{1,9},{2,10},{3,11},{4,12},{5,13},{6,14},{7,15},{8,0},{9,1},... | collective-permute-start | bytes 12296 | tf_op jit(solution)/shard_map/ppermute | solution.py:78

commit v6 on v4

--- a/solution.py
+++ b/solution.py
@@ -7,7 +7,7 @@
 from jax.experimental.pallas import tpu as pltpu
 from jax.sharding import PartitionSpec as P
 
-ROW_TILE = 512
+ROW_TILE = 1024
 
 
 def fused_kernel(obs_ref, gathered_ref, khatri_ref, node_ref, contracted_ref):
@@ -22,8 +22,8 @@
         jnp.bfloat16
     )
     node = lax.dot_general(
-        khatri, derivative, (((1,), (1,)), ((), ())), preferred_element_type=jnp.float32
-    )
+        derivative, khatri, (((1,), (1,)), ((), ())), preferred_element_type=jnp.float32
+    ).T
     for c in range(pieces):
         node_ref[c] = node[:, c * piece : (c + 1) * piece]
     part = jnp.dot(factor, derivative, preferred_element_type=jnp.float32)

time: 87.5 us -> 85.9 us (0.982)
  Pallas kernels: 11.4 us -> 9.98 us
    pallas_call x1, Pallas kernels: 11.4 us -> 9.98 us  [fused(): pl.pallas_call(fused_kernel, grid=(rows // tile,), in_specs=[pl.BlockSpec...]
where the time goes in v6:
time: 85.9 us; the launch traced here: 85.5 us
  waiting for transfers between devices  38 us (44%)
  starting transfers between devices  28.7 us (33%)
  Pallas kernels  9.98 us (12%)
  local copies, waits for them, and re-layouts  5.84 us (7%)
  other arithmetic  2.27 us (3%)
    ppermute x8, waiting for transfers between devices, butterfly_sum(): values = values + lax.ppermute(values, axis, pairs)  25.1 us
    ppermute x8, starting transfers between devices, butterfly_sum(): values = values + lax.ppermute(values, axis, pairs)  13.2 us
    all_to_all x1, waiting for transfers between devices, gather_blocks(): return lax.all_to_all(copies, axis, 0, 0, tiled=True)  12.9 us
    pallas_call x1, Pallas kernels, fused(): pl.pallas_call(fused_kernel, grid=(rows // tile,), in_specs=[pl.BlockSpec...  9.98 us
    all_to_all x1, starting transfers between devices, gather_blocks(): return lax.all_to_all(copies, axis, 0, 0, tiled=True)  9.94 us
    all_to_all x1, starting transfers between devices, shards(): summed = lax.all_to_all(blocks, 'tm', 0, 0, tiled=True).sum(0)  5.6 us
  transfers between devices with their start and end apart: 10, of which 9 were waited for; matrix products, arithmetic and copies ran while one was open for 6% of the time, Pallas kernels for 0%

profile of v6, /device:TPU:22, one launch (start us, length us, event | category | flops | bytes accessed | tf_op | source)
XLA Modules:
  0.0 85.5 jit_solution(8545755835648118174)
XLA Ops:
  0.6 1.6 %broadcast_in_dim.2 = bf16[16,64,256]{2,1,0:T(8,128)(2,1)} broadcast(bf16[64,256]{1,0:T(8,128)(2,1)} %param.5), dimensions={1,2} | broadcast | bytes 557056 | tf_op jit(solution)/shard_map/broadcast_in_dim | solution.py:67
  2.2 9.9 %all-to-all-start = ((bf16[16,64,256]{2,1,0:T(8,128)(2,1)}), bf16[16,64,256]{2,1,0:T(8,128)(2,1)S(1)}, u32[]{:S(2)}, u32[]{:S(2)}) async-start(bf16[16,64,256]{2,1,0:T(8,128)(2,1)} %broadcast_in_dim.2), calls=%async_computation | async-start | bytes 1048576 | tf_op jit(solution)/shard_map/all_to_all | solution.py:68
  12.2 0.8 copy.9
  13.0 0.7 convert_element_type.12
  13.7 0.1 multiply_convert_fusion
  13.7 0.8 copy.10.khatri_ref
  14.5 12.9 %all-to-all-done.gathered_ref = bf16[16,64,256]{2,1,0:T(8,128)(2,1)S(1)} async-done(((bf16[16,64,256]{2,1,0:T(8,128)(2,1)}), bf16[16,64,256]{2,1,0:T(8,128)(2,1)S(1)}, u32[]{:S(2)}, u32[]{:S(2)}) %all-to-all-start) | async-done | bytes 524320 | tf_op jit(solution)/shard_map/all_to_all | solution.py:68
  27.4 0.8 copy-done
  28.2 10.0 %shard_map.67 = (f32[16,64,256]{2,1,0:T(8,128)}, f32[64,1024]{1,0:T(8,128)}) custom-call(bf16[4096,1024]{1,0:T(8,128)(2,1)} %obs_ref.1, bf16[16,64,256]{2,1,0:T(8,128)(2,1)} %copy-done, bf16[64,1024]{1,0:T(8,128)(2,1)} %copy.10.khatri_ref), custom_call_target="tpu_custom_call" | custom-call | tf_op jit(solution)/shard_map/pallas_call | solution.py:45
  38.2 5.6 %all-to-all-start.1 = ((f32[16,64,256]{2,1,0:T(8,128)}), f32[16,64,256]{2,1,0:T(8,128)S(1)}, u32[]{:S(2)}, u32[]{:S(2)}) async-start(f32[16,64,256]{2,1,0:T(8,128)} %get-tuple-element.5), calls=%async_computation.1 | async-start | bytes 2097152 | tf_op jit(solution)/shard_map/all_to_all | solution.py:109
  43.8 1.1 %copy.11 = f32[64,1024]{0,1:T(8,128)S(1)} copy(f32[64,1024]{1,0:T(8,128)} %get-tuple-element.6) | data formatting | bytes 524288 | tf_op jit(solution)/shard_map/pallas_call | solution.py:45
  45.0 0.2 multiply_reduce_fusion
  45.1 0.1 collective-permute-start
  45.2 1.2 %collective-permute-done = f32[64,80]{0,1:T(8,128)S(1)} collective-permute-done((f32[64,80]{0,1:T(8,128)S(1)}, f32[64,80]{0,1:T(8,128)S(1)}, u32[]{:S(2)}, u32[]{:S(2)}) %collective-permute-start) | collective-permute-done | bytes 20512 | tf_op jit(solution)/shard_map/ppermute | solution.py:76
  46.5 1.5 %collective-permute-start.1 = (f32[64,80]{0,1:T(8,128)S(1)}, f32[64,80]{0,1:T(8,128)S(1)}, u32[]{:S(2)}, u32[]{:S(2)}) collective-permute-start(f32[64,80]{0,1:T(8,128)S(1)} %fusion), channel_id=1, source_target_pairs={{0,32},{16,48},{32,0},{48,16},{64,96},{80,112},{96,64},{112,80},{1... | collective-permute-start | bytes 61448 | tf_op jit(solution)/shard_map/ppermute | solution.py:76
  48.0 4.3 %collective-permute-done.1 = f32[64,80]{0,1:T(8,128)S(1)} collective-permute-done((f32[64,80]{0,1:T(8,128)S(1)}, f32[64,80]{0,1:T(8,128)S(1)}, u32[]{:S(2)}, u32[]{:S(2)}) %collective-permute-start.1) | collective-permute-done | bytes 20512 | tf_op jit(solution)/shard_map/ppermute | solution.py:76
  52.3 1.3 %collective-permute-start.2 = (f32[64,80]{0,1:T(8,128)S(1)}, f32[64,80]{0,1:T(8,128)S(1)}, u32[]{:S(2)}, u32[]{:S(2)}) collective-permute-start(f32[64,80]{0,1:T(8,128)S(1)} %add.25), channel_id=1, source_target_pairs={{0,64},{16,80},{32,96},{48,112},{64,0},{80,16},{96,32},{112,48},{1... | collective-permute-start | bytes 61448 | tf_op jit(solution)/shard_map/ppermute | solution.py:76
  53.6 2.7 %collective-permute-done.2 = f32[64,80]{0,1:T(8,128)S(1)} collective-permute-done((f32[64,80]{0,1:T(8,128)S(1)}, f32[64,80]{0,1:T(8,128)S(1)}, u32[]{:S(2)}, u32[]{:S(2)}) %collective-permute-start.2) | collective-permute-done | bytes 20512 | tf_op jit(solution)/shard_map/ppermute | solution.py:76
  56.3 0.3 collective-permute-start.3
  56.6 5.2 %collective-permute-done.3 = f32[64,80]{0,1:T(8,128)S(1)} collective-permute-done((f32[64,80]{0,1:T(8,128)S(1)}, f32[64,80]{0,1:T(8,128)S(1)}, u32[]{:S(2)}, u32[]{:S(2)}) %collective-permute-start.3) | collective-permute-done | bytes 20512 | tf_op jit(solution)/shard_map/ppermute | solution.py:76
  61.8 0.2 collective-permute-start.4
  62.0 4.0 %collective-permute-done.4 = f32[64,16]{0,1:T(8,128)S(1)} collective-permute-done((f32[64,16]{0,1:T(8,128)S(1)}, f32[64,16]{0,1:T(8,128)S(1)}, u32[]{:S(2)}, u32[]{:S(2)}) %collective-permute-start.4) | collective-permute-done | bytes 4128 | tf_op jit(solution)/shard_map/ppermute | solution.py:76
  66.0 2.4 %collective-permute-start.5 = (f32[64,16]{0,1:T(8,128)S(1)}, f32[64,16]{0,1:T(8,128)S(1)}, u32[]{:S(2)}, u32[]{:S(2)}) collective-permute-start(f32[64,16]{0,1:T(8,128)S(1)} %slice_add_fusion), channel_id=1, source_target_pairs={{0,2},{1,3},{2,0},{3,1},{4,6},{5,7},{6,4},{7,5},{8,10},{9,11},{10,... | collective-permute-start | bytes 12296 | tf_op jit(solution)/shard_map/ppermute | solution.py:76
  68.5 1.6 %collective-permute-done.5 = f32[64,16]{0,1:T(8,128)S(1)} collective-permute-done((f32[64,16]{0,1:T(8,128)S(1)}, f32[64,16]{0,1:T(8,128)S(1)}, u32[]{:S(2)}, u32[]{:S(2)}) %collective-permute-start.5) | collective-permute-done | bytes 4128 | tf_op jit(solution)/shard_map/ppermute | solution.py:76
  70.1 4.8 %collective-permute-start.6 = (f32[64,16]{0,1:T(8,128)S(1)}, f32[64,16]{0,1:T(8,128)S(1)}, u32[]{:S(2)}, u32[]{:S(2)}) collective-permute-start(f32[64,16]{0,1:T(8,128)S(1)} %add.29), channel_id=1, source_target_pairs={{0,4},{1,5},{2,6},{3,7},{4,0},{5,1},{6,2},{7,3},{8,12},{9,13},{10,... | collective-permute-start | bytes 12296 | tf_op jit(solution)/shard_map/ppermute | solution.py:76
  74.9 1.7 %collective-permute-done.6 = f32[64,16]{0,1:T(8,128)S(1)} collective-permute-done((f32[64,16]{0,1:T(8,128)S(1)}, f32[64,16]{0,1:T(8,128)S(1)}, u32[]{:S(2)}, u32[]{:S(2)}) %collective-permute-start.6) | collective-permute-done | bytes 4128 | tf_op jit(solution)/shard_map/ppermute | solution.py:76
  76.6 2.5 %collective-permute-start.7 = (f32[64,16]{0,1:T(8,128)S(1)}, f32[64,16]{0,1:T(8,128)S(1)}, u32[]{:S(2)}, u32[]{:S(2)}) collective-permute-start(f32[64,16]{0,1:T(8,128)S(1)} %add.30), channel_id=1, source_target_pairs={{0,8},{1,9},{2,10},{3,11},{4,12},{5,13},{6,14},{7,15},{8,0},{9,1},... | collective-permute-start | bytes 12296 | tf_op jit(solution)/shard_map/ppermute | solution.py:76
  79.1 0.7 copy.12
  79.8 4.3 %collective-permute-done.7 = f32[64,16]{0,1:T(8,128)S(1)} collective-permute-done((f32[64,16]{0,1:T(8,128)S(1)}, f32[64,16]{0,1:T(8,128)S(1)}, u32[]{:S(2)}, u32[]{:S(2)}) %collective-permute-start.7) | collective-permute-done | bytes 4128 | tf_op jit(solution)/shard_map/ppermute | solution.py:76
  84.2 0.6 add_multiply_fusion
  84.8 0.1 reduce_sum.27
  84.8 0.6 broadcast_multiply_fusion
  (12 shorter events, 0.1 us)
Async XLA Ops:
  2.2 25.2 %all-to-all-start = ((bf16[16,64,256]{2,1,0:T(8,128)(2,1)}), bf16[16,64,256]{2,1,0:T(8,128)(2,1)S(1)}, u32[]{:S(2)}, u32[]{:S(2)}) async-start(bf16[16,64,256]{2,1,0:T(8,128)(2,1)} %broadcast_in_dim.2), calls=%async_computation | async-start | bytes 1048576 | tf_op jit(solution)/shard_map/all_to_all | solution.py:68
  27.4 0.8 copy-start
  38.2 46.6 %all-to-all-start.1 = ((f32[16,64,256]{2,1,0:T(8,128)}), f32[16,64,256]{2,1,0:T(8,128)S(1)}, u32[]{:S(2)}, u32[]{:S(2)}) async-start(f32[16,64,256]{2,1,0:T(8,128)} %get-tuple-element.5), calls=%async_computation.1 | async-start | bytes 2097152 | tf_op jit(solution)/shard_map/all_to_all | solution.py:109
  45.1 1.3 %collective-permute-start = (f32[64,80]{0,1:T(8,128)S(1)}, f32[64,80]{0,1:T(8,128)S(1)}, u32[]{:S(2)}, u32[]{:S(2)}) collective-permute-start(f32[64,80]{0,1:T(8,128)S(1)} %pad_maximum_fusion), channel_id=1, source_target_pairs={{0,16},{16,0},{32,48},{48,32},{64,80},{80,64},{96,112},{112,96},{1... | collective-permute-start | bytes 61448 | tf_op jit(solution)/shard_map/ppermute | solution.py:76
  46.5 5.8 %collective-permute-start.1 = (f32[64,80]{0,1:T(8,128)S(1)}, f32[64,80]{0,1:T(8,128)S(1)}, u32[]{:S(2)}, u32[]{:S(2)}) collective-permute-start(f32[64,80]{0,1:T(8,128)S(1)} %fusion), channel_id=1, source_target_pairs={{0,32},{16,48},{32,0},{48,16},{64,96},{80,112},{96,64},{112,80},{1... | collective-permute-start | bytes 61448 | tf_op jit(solution)/shard_map/ppermute | solution.py:76
  52.3 4.0 %collective-permute-start.2 = (f32[64,80]{0,1:T(8,128)S(1)}, f32[64,80]{0,1:T(8,128)S(1)}, u32[]{:S(2)}, u32[]{:S(2)}) collective-permute-start(f32[64,80]{0,1:T(8,128)S(1)} %add.25), channel_id=1, source_target_pairs={{0,64},{16,80},{32,96},{48,112},{64,0},{80,16},{96,32},{112,48},{1... | collective-permute-start | bytes 61448 | tf_op jit(solution)/shard_map/ppermute | solution.py:76
  56.3 5.5 %collective-permute-start.3 = (f32[64,80]{0,1:T(8,128)S(1)}, f32[64,80]{0,1:T(8,128)S(1)}, u32[]{:S(2)}, u32[]{:S(2)}) collective-permute-start(f32[64,80]{0,1:T(8,128)S(1)} %add.26), channel_id=1, source_target_pairs={{0,128},{16,144},{32,160},{48,176},{64,192},{80,208},{96,224},{112... | collective-permute-start | bytes 61448 | tf_op jit(solution)/shard_map/ppermute | solution.py:76
  61.8 4.2 %collective-permute-start.4 = (f32[64,16]{0,1:T(8,128)S(1)}, f32[64,16]{0,1:T(8,128)S(1)}, u32[]{:S(2)}, u32[]{:S(2)}) collective-permute-start(f32[64,16]{0,1:T(8,128)S(1)} %slice.9), channel_id=1, source_target_pairs={{0,1},{1,0},{2,3},{3,2},{4,5},{5,4},{6,7},{7,6},{8,9},{9,8},{10,11... | collective-permute-start | bytes 12296 | tf_op jit(solution)/shard_map/ppermute | solution.py:76
  66.0 4.1 %collective-permute-start.5 = (f32[64,16]{0,1:T(8,128)S(1)}, f32[64,16]{0,1:T(8,128)S(1)}, u32[]{:S(2)}, u32[]{:S(2)}) collective-permute-start(f32[64,16]{0,1:T(8,128)S(1)} %slice_add_fusion), channel_id=1, source_target_pairs={{0,2},{1,3},{2,0},{3,1},{4,6},{5,7},{6,4},{7,5},{8,10},{9,11},{10,... | collective-permute-start | bytes 12296 | tf_op jit(solution)/shard_map/ppermute | solution.py:76
  70.1 6.5 %collective-permute-start.6 = (f32[64,16]{0,1:T(8,128)S(1)}, f32[64,16]{0,1:T(8,128)S(1)}, u32[]{:S(2)}, u32[]{:S(2)}) collective-permute-start(f32[64,16]{0,1:T(8,128)S(1)} %add.29), channel_id=1, source_target_pairs={{0,4},{1,5},{2,6},{3,7},{4,0},{5,1},{6,2},{7,3},{8,12},{9,13},{10,... | collective-permute-start | bytes 12296 | tf_op jit(solution)/shard_map/ppermute | solution.py:76
  76.6 7.6 %collective-permute-start.7 = (f32[64,16]{0,1:T(8,128)S(1)}, f32[64,16]{0,1:T(8,128)S(1)}, u32[]{:S(2)}, u32[]{:S(2)}) collective-permute-start(f32[64,16]{0,1:T(8,128)S(1)} %add.30), channel_id=1, source_target_pairs={{0,8},{1,9},{2,10},{3,11},{4,12},{5,13},{6,14},{7,15},{8,0},{9,1},... | collective-permute-start | bytes 12296 | tf_op jit(solution)/shard_map/ppermute | solution.py:76

commit v7 on v6

--- a/solution.py
+++ b/solution.py
@@ -96,9 +96,13 @@
     )
     gathered = gather_blocks(node_factor, "tm")
     blocks, contracted_t = fused(observed, gathered, khatri)
-    by_step = contracted_t.reshape(factor_rank, time_dev, species)
-    time_part = (by_step * species_vals[:, None, :]).sum(2)
-    species_part = (by_step * time_vals[:, :, None]).sum(1)
+    column = jnp.arange(flat_width)
+    step_of = (column[:, None] // species == jnp.arange(time_dev)[None, :]).astype(jnp.float32)
+    species_of = (column[:, None] % species == jnp.arange(species)[None, :]).astype(jnp.float32)
+    species_wide = jnp.tile(species_vals, (1, time_dev))
+    time_wide = jnp.repeat(time_vals, species, axis=1)
+    time_part = jnp.dot(contracted_t * species_wide, step_of, precision=lax.Precision.HIGHEST)
+    species_part = jnp.dot(contracted_t * time_wide, species_of, precision=lax.Precision.HIGHEST)
 
     small = jnp.concatenate([time_part, species_part], axis=1)
     small_sum = butterfly_sum(small, "node")

time: 85.9 us -> 88.2 us (1.027)
  starting transfers between devices: 28.7 us -> 25.4 us
  waiting for transfers between devices: 38 us -> 41 us
  matrix products: 0 us -> 2.75 us
    ppermute x8, waiting for transfers between devices: 25.1 us -> 28.4 us  [butterfly_sum(): values = values + lax.ppermute(values, axis, pairs)]
    ppermute x8, starting transfers between devices: 13.2 us -> 9.87 us  [butterfly_sum(): values = values + lax.ppermute(values, axis, pairs)]
    dot_general x0 -> x2, matrix products: none -> 2.75 us  [the longest x1 1.38 us: shards(): jnp.dot(contracted_t * species_wide, step_of, precision=lax.Precision.HIG...]
    pallas_call x1 -> x0, local copies, waits for them, and re-layouts: 1.14 us -> none  [fused(): pl.pallas_call(fused_kernel, grid=(rows // tile,), in_specs=[pl.BlockSpec...]
    mul x0 -> x4, local copies, waits for them, and re-layouts: none -> 1.12 us  [shards(): time_vals[:, :, None] * species_vals[:, None, :]]
  transfers between devices with their start and end apart: 10 -> 10, of which waited for: 9 -> 9; matrix products, arithmetic and copies ran while one was open for 6% -> 8% of each run, Pallas kernels for 0% -> 0%
where the time goes in v7:
time: 88.2 us; the launch traced here: 87.2 us
  waiting for transfers between devices  41 us (46%)
  starting transfers between devices  25.4 us (29%)
  Pallas kernels  10 us (11%)
  local copies, waits for them, and re-layouts  5.07 us (6%)
  matrix products  2.75 us (3%)
  other arithmetic  2.27 us (3%)
    ppermute x8, waiting for transfers between devices, butterfly_sum(): values = values + lax.ppermute(values, axis, pairs)  28.4 us
    all_to_all x1, waiting for transfers between devices, gather_blocks(): return lax.all_to_all(copies, axis, 0, 0, tiled=True)  12.6 us
    pallas_call x1, Pallas kernels, fused(): pl.pallas_call(fused_kernel, grid=(rows // tile,), in_specs=[pl.BlockSpec...  10 us
    all_to_all x1, starting transfers between devices, gather_blocks(): return lax.all_to_all(copies, axis, 0, 0, tiled=True)  9.94 us
    ppermute x8, starting transfers between devices, butterfly_sum(): values = values + lax.ppermute(values, axis, pairs)  9.87 us
    all_to_all x1, starting transfers between devices, shards(): summed = lax.all_to_all(blocks, 'tm', 0, 0, tiled=True).sum(0)  5.6 us
  transfers between devices with their start and end apart: 10, of which 9 were waited for; matrix products, arithmetic and copies ran while one was open for 8% of the time, Pallas kernels for 0%

profile of v7, /device:TPU:22, one launch (start us, length us, event | category | flops | bytes accessed | tf_op | source)
XLA Modules:
  0.0 87.2 jit_solution(5015988290437424289)
XLA Ops:
  0.6 1.6 %broadcast_in_dim.2 = bf16[16,64,256]{2,1,0:T(8,128)(2,1)} broadcast(bf16[64,256]{1,0:T(8,128)(2,1)} %param.5), dimensions={1,2} | broadcast | bytes 557056 | tf_op jit(solution)/shard_map/broadcast_in_dim | solution.py:67
  2.2 9.9 %all-to-all-start = ((bf16[16,64,256]{2,1,0:T(8,128)(2,1)}), bf16[16,64,256]{2,1,0:T(8,128)(2,1)S(1)}, u32[]{:S(2)}, u32[]{:S(2)}) async-start(bf16[16,64,256]{2,1,0:T(8,128)(2,1)} %broadcast_in_dim.2), calls=%async_computation | async-start | bytes 1048576 | tf_op jit(solution)/shard_map/all_to_all | solution.py:68
  12.2 0.8 copy.10
  13.0 0.2 copy.11
  13.2 0.7 mul.26
  13.9 0.2 copy.12
  14.1 0.7 multiply_convert_fusion.khatri_ref
  14.8 12.6 %all-to-all-done.gathered_ref = bf16[16,64,256]{2,1,0:T(8,128)(2,1)S(1)} async-done(((bf16[16,64,256]{2,1,0:T(8,128)(2,1)}), bf16[16,64,256]{2,1,0:T(8,128)(2,1)S(1)}, u32[]{:S(2)}, u32[]{:S(2)}) %all-to-all-start) | async-done | bytes 524320 | tf_op jit(solution)/shard_map/all_to_all | solution.py:68
  27.4 0.8 copy-done
  28.2 10.0 %shard_map.67 = (f32[16,64,256]{2,1,0:T(8,128)}, f32[64,1024]{1,0:T(8,128)}) custom-call(bf16[4096,1024]{1,0:T(8,128)(2,1)} %obs_ref.1, bf16[16,64,256]{2,1,0:T(8,128)(2,1)} %copy-done, bf16[64,1024]{1,0:T(8,128)(2,1)} %multiply_convert_fusion.khatri_ref), custom_call_target="tpu_custom_call" | custom-call | tf_op jit(solution)/shard_map/pallas_call | solution.py:45
  38.2 5.6 %all-to-all-start.1 = ((f32[16,64,256]{2,1,0:T(8,128)}), f32[16,64,256]{2,1,0:T(8,128)S(1)}, u32[]{:S(2)}, u32[]{:S(2)}) async-start(f32[16,64,256]{2,1,0:T(8,128)} %get-tuple-element.5), calls=%async_computation.1 | async-start | bytes 2097152 | tf_op jit(solution)/shard_map/all_to_all | solution.py:113
  43.8 1.4 %fusion = f32[64,64]{1,0:T(8,128)S(1)} fusion(s32[1024]{0:T(1024)S(1)} %add_select_fusion, f32[64,1024]{1,0:T(8,128)} %get-tuple-element.6, f32[64,1024]{1,0:T(8,128)S(1)} %copy.12), kind=kOutput, calls=%fused_computation.2 | convolution fusion | flops 50462720 | bytes 544768 | tf_op jit(solution)/shard_map/dot_general | solution.py:104
  45.2 1.4 %fusion.1 = f32[64,16]{1,0:T(8,128)S(1)} fusion(s32[1024]{0:T(1024)S(1)} %fusion.6, f32[64,1024]{1,0:T(8,128)} %get-tuple-element.6, f32[64,1024]{1,0:T(8,128)S(1)} %copy.11), kind=kOutput, calls=%fused_computation.3 | convolution fusion | flops 12664832 | bytes 532480 | tf_op jit(solution)/shard_map/dot_general | solution.py:105
  46.6 0.1 pad_maximum_fusion
  46.7 1.2 %collective-permute-done = f32[64,80]{1,0:T(8,128)S(1)} collective-permute-done((f32[64,80]{1,0:T(8,128)S(1)}, f32[64,80]{1,0:T(8,128)S(1)}, u32[]{:S(2)}, u32[]{:S(2)}) %collective-permute-start) | collective-permute-done | bytes 20512 | tf_op jit(solution)/shard_map/ppermute | solution.py:76
  48.0 1.4 %collective-permute-start.1 = (f32[64,80]{1,0:T(8,128)S(1)}, f32[64,80]{1,0:T(8,128)S(1)}, u32[]{:S(2)}, u32[]{:S(2)}) collective-permute-start(f32[64,80]{1,0:T(8,128)S(1)} %fusion.13), channel_id=1, source_target_pairs={{0,32},{16,48},{32,0},{48,16},{64,96},{80,112},{96,64},{112,80},{1... | collective-permute-start | bytes 61448 | tf_op jit(solution)/shard_map/ppermute | solution.py:76
  49.4 4.1 %collective-permute-done.1 = f32[64,80]{1,0:T(8,128)S(1)} collective-permute-done((f32[64,80]{1,0:T(8,128)S(1)}, f32[64,80]{1,0:T(8,128)S(1)}, u32[]{:S(2)}, u32[]{:S(2)}) %collective-permute-start.1) | collective-permute-done | bytes 20512 | tf_op jit(solution)/shard_map/ppermute | solution.py:76
  53.6 1.3 %collective-permute-start.2 = (f32[64,80]{1,0:T(8,128)S(1)}, f32[64,80]{1,0:T(8,128)S(1)}, u32[]{:S(2)}, u32[]{:S(2)}) collective-permute-start(f32[64,80]{1,0:T(8,128)S(1)} %add.43), channel_id=1, source_target_pairs={{0,64},{16,80},{32,96},{48,112},{64,0},{80,16},{96,32},{112,48},{1... | collective-permute-start | bytes 61448 | tf_op jit(solution)/shard_map/ppermute | solution.py:76
  54.9 2.6 %collective-permute-done.2 = f32[64,80]{1,0:T(8,128)S(1)} collective-permute-done((f32[64,80]{1,0:T(8,128)S(1)}, f32[64,80]{1,0:T(8,128)S(1)}, u32[]{:S(2)}, u32[]{:S(2)}) %collective-permute-start.2) | collective-permute-done | bytes 20512 | tf_op jit(solution)/shard_map/ppermute | solution.py:76
  57.5 0.3 collective-permute-start.3
  57.8 5.1 %collective-permute-done.3 = f32[64,80]{1,0:T(8,128)S(1)} collective-permute-done((f32[64,80]{1,0:T(8,128)S(1)}, f32[64,80]{1,0:T(8,128)S(1)}, u32[]{:S(2)}, u32[]{:S(2)}) %collective-permute-start.3) | collective-permute-done | bytes 20512 | tf_op jit(solution)/shard_map/ppermute | solution.py:76
  63.0 0.2 collective-permute-start.4
  63.2 5.9 %collective-permute-done.4 = f32[64,16]{1,0:T(8,128)S(1)} collective-permute-done((f32[64,16]{1,0:T(8,128)S(1)}, f32[64,16]{1,0:T(8,128)S(1)}, u32[]{:S(2)}, u32[]{:S(2)}) %collective-permute-start.4) | collective-permute-done | bytes 4128 | tf_op jit(solution)/shard_map/ppermute | solution.py:76
  69.2 0.7 collective-permute-start.5
  69.9 3.3 %collective-permute-done.5 = f32[64,16]{1,0:T(8,128)S(1)} collective-permute-done((f32[64,16]{1,0:T(8,128)S(1)}, f32[64,16]{1,0:T(8,128)S(1)}, u32[]{:S(2)}, u32[]{:S(2)}) %collective-permute-start.5) | collective-permute-done | bytes 4128 | tf_op jit(solution)/shard_map/ppermute | solution.py:76
  73.2 2.4 %collective-permute-start.6 = (f32[64,16]{1,0:T(8,128)S(1)}, f32[64,16]{1,0:T(8,128)S(1)}, u32[]{:S(2)}, u32[]{:S(2)}) collective-permute-start(f32[64,16]{1,0:T(8,128)S(1)} %add.47), channel_id=1, source_target_pairs={{0,4},{1,5},{2,6},{3,7},{4,0},{5,1},{6,2},{7,3},{8,12},{9,13},{10,... | collective-permute-start | bytes 12296 | tf_op jit(solution)/shard_map/ppermute | solution.py:76
  75.5 2.4 %collective-permute-done.6 = f32[64,16]{1,0:T(8,128)S(1)} collective-permute-done((f32[64,16]{1,0:T(8,128)S(1)}, f32[64,16]{1,0:T(8,128)S(1)}, u32[]{:S(2)}, u32[]{:S(2)}) %collective-permute-start.6) | collective-permute-done | bytes 4128 | tf_op jit(solution)/shard_map/ppermute | solution.py:76
  78.0 3.5 %collective-permute-start.7 = (f32[64,16]{1,0:T(8,128)S(1)}, f32[64,16]{1,0:T(8,128)S(1)}, u32[]{:S(2)}, u32[]{:S(2)}) collective-permute-start(f32[64,16]{1,0:T(8,128)S(1)} %add.48), channel_id=1, source_target_pairs={{0,8},{1,9},{2,10},{3,11},{4,12},{5,13},{6,14},{7,15},{8,0},{9,1},... | collective-permute-start | bytes 12296 | tf_op jit(solution)/shard_map/ppermute | solution.py:76
  81.5 0.6 slice_multiply_fusion
  82.1 3.7 %collective-permute-done.7 = f32[64,16]{1,0:T(8,128)S(1)} collective-permute-done((f32[64,16]{1,0:T(8,128)S(1)}, f32[64,16]{1,0:T(8,128)S(1)}, u32[]{:S(2)}, u32[]{:S(2)}) %collective-permute-start.7) | collective-permute-done | bytes 4128 | tf_op jit(solution)/shard_map/ppermute | solution.py:76
  85.8 0.7 copy.16
  86.6 0.6 broadcast_multiply_fusion
  (16 shorter events, 0.4 us)
Async XLA Ops:
  2.2 25.2 %all-to-all-start = ((bf16[16,64,256]{2,1,0:T(8,128)(2,1)}), bf16[16,64,256]{2,1,0:T(8,128)(2,1)S(1)}, u32[]{:S(2)}, u32[]{:S(2)}) async-start(bf16[16,64,256]{2,1,0:T(8,128)(2,1)} %broadcast_in_dim.2), calls=%async_computation | async-start | bytes 1048576 | tf_op jit(solution)/shard_map/all_to_all | solution.py:68
  27.4 0.8 copy-start
  38.2 48.3 %all-to-all-start.1 = ((f32[16,64,256]{2,1,0:T(8,128)}), f32[16,64,256]{2,1,0:T(8,128)S(1)}, u32[]{:S(2)}, u32[]{:S(2)}) async-start(f32[16,64,256]{2,1,0:T(8,128)} %get-tuple-element.5), calls=%async_computation.1 | async-start | bytes 2097152 | tf_op jit(solution)/shard_map/all_to_all | solution.py:113
  46.7 1.2 %collective-permute-start = (f32[64,80]{1,0:T(8,128)S(1)}, f32[64,80]{1,0:T(8,128)S(1)}, u32[]{:S(2)}, u32[]{:S(2)}) collective-permute-start(f32[64,80]{1,0:T(8,128)S(1)} %pad_maximum_fusion), channel_id=1, source_target_pairs={{0,16},{16,0},{32,48},{48,32},{64,80},{80,64},{96,112},{112,96},{1... | collective-permute-start | bytes 61448 | tf_op jit(solution)/shard_map/ppermute | solution.py:76
  48.0 5.6 %collective-permute-start.1 = (f32[64,80]{1,0:T(8,128)S(1)}, f32[64,80]{1,0:T(8,128)S(1)}, u32[]{:S(2)}, u32[]{:S(2)}) collective-permute-start(f32[64,80]{1,0:T(8,128)S(1)} %fusion.13), channel_id=1, source_target_pairs={{0,32},{16,48},{32,0},{48,16},{64,96},{80,112},{96,64},{112,80},{1... | collective-permute-start | bytes 61448 | tf_op jit(solution)/shard_map/ppermute | solution.py:76
  53.6 3.9 %collective-permute-start.2 = (f32[64,80]{1,0:T(8,128)S(1)}, f32[64,80]{1,0:T(8,128)S(1)}, u32[]{:S(2)}, u32[]{:S(2)}) collective-permute-start(f32[64,80]{1,0:T(8,128)S(1)} %add.43), channel_id=1, source_target_pairs={{0,64},{16,80},{32,96},{48,112},{64,0},{80,16},{96,32},{112,48},{1... | collective-permute-start | bytes 61448 | tf_op jit(solution)/shard_map/ppermute | solution.py:76
  57.5 5.4 %collective-permute-start.3 = (f32[64,80]{1,0:T(8,128)S(1)}, f32[64,80]{1,0:T(8,128)S(1)}, u32[]{:S(2)}, u32[]{:S(2)}) collective-permute-start(f32[64,80]{1,0:T(8,128)S(1)} %add.44), channel_id=1, source_target_pairs={{0,128},{16,144},{32,160},{48,176},{64,192},{80,208},{96,224},{112... | collective-permute-start | bytes 61448 | tf_op jit(solution)/shard_map/ppermute | solution.py:76
  63.0 6.1 %collective-permute-start.4 = (f32[64,16]{1,0:T(8,128)S(1)}, f32[64,16]{1,0:T(8,128)S(1)}, u32[]{:S(2)}, u32[]{:S(2)}) collective-permute-start(f32[64,16]{1,0:T(8,128)S(1)} %slice.9), channel_id=1, source_target_pairs={{0,1},{1,0},{2,3},{3,2},{4,5},{5,4},{6,7},{7,6},{8,9},{9,8},{10,11... | collective-permute-start | bytes 12296 | tf_op jit(solution)/shard_map/ppermute | solution.py:76
  69.2 3.9 %collective-permute-start.5 = (f32[64,16]{1,0:T(8,128)S(1)}, f32[64,16]{1,0:T(8,128)S(1)}, u32[]{:S(2)}, u32[]{:S(2)}) collective-permute-start(f32[64,16]{1,0:T(8,128)S(1)} %slice_add_fusion), channel_id=1, source_target_pairs={{0,2},{1,3},{2,0},{3,1},{4,6},{5,7},{6,4},{7,5},{8,10},{9,11},{10,... | collective-permute-start | bytes 12296 | tf_op jit(solution)/shard_map/ppermute | solution.py:76
  73.2 4.8 %collective-permute-start.6 = (f32[64,16]{1,0:T(8,128)S(1)}, f32[64,16]{1,0:T(8,128)S(1)}, u32[]{:S(2)}, u32[]{:S(2)}) collective-permute-start(f32[64,16]{1,0:T(8,128)S(1)} %add.47), channel_id=1, source_target_pairs={{0,4},{1,5},{2,6},{3,7},{4,0},{5,1},{6,2},{7,3},{8,12},{9,13},{10,... | collective-permute-start | bytes 12296 | tf_op jit(solution)/shard_map/ppermute | solution.py:76
  78.0 7.9 %collective-permute-start.7 = (f32[64,16]{1,0:T(8,128)S(1)}, f32[64,16]{1,0:T(8,128)S(1)}, u32[]{:S(2)}, u32[]{:S(2)}) collective-permute-start(f32[64,16]{1,0:T(8,128)S(1)} %add.48), channel_id=1, source_target_pairs={{0,8},{1,9},{2,10},{3,11},{4,12},{5,13},{6,14},{7,15},{8,0},{9,1},... | collective-permute-start | bytes 12296 | tf_op jit(solution)/shard_map/ppermute | solution.py:76

commit v8 on v7

--- a/solution.py
+++ b/solution.py
@@ -10,7 +10,10 @@
 ROW_TILE = 1024
 
 
-def fused_kernel(obs_ref, gathered_ref, khatri_ref, node_ref, contracted_ref):
+def fused_kernel(
+    obs_ref, gathered_ref, khatri_ref, species_wide_ref, time_wide_ref,
+    node_ref, time_ref, species_ref, contracted_ref,
+):
     step = pl.program_id(0)
     pieces, _, piece = gathered_ref.shape
     khatri = khatri_ref[...]
@@ -36,8 +39,27 @@
     def _():
         contracted_ref[...] += part
 
+    @pl.when(step == pl.num_programs(0) - 1)
+    def _():
+        contracted = contracted_ref[...]
+        width = contracted.shape[1]
+        steps = time_ref.shape[1]
+        kinds = species_ref.shape[1]
+        column = lax.broadcasted_iota(jnp.int32, (width, steps), 0)
+        step_of = (column // kinds == lax.broadcasted_iota(jnp.int32, (width, steps), 1))
+        column = lax.broadcasted_iota(jnp.int32, (width, kinds), 0)
+        kind_of = (column % kinds == lax.broadcasted_iota(jnp.int32, (width, kinds), 1))
+        time_ref[...] = jnp.dot(
+            contracted * species_wide_ref[...], step_of.astype(jnp.float32),
+            precision=lax.Precision.HIGHEST, preferred_element_type=jnp.float32,
+        )
+        species_ref[...] = jnp.dot(
+            contracted * time_wide_ref[...], kind_of.astype(jnp.float32),
+            precision=lax.Precision.HIGHEST, preferred_element_type=jnp.float32,
+        )
 
-def fused(observed, gathered, khatri):
+
+def fused(observed, gathered, khatri, species_wide, time_wide, steps, kinds):
     rows, width = observed.shape
     count, rank, piece = gathered.shape
     tile = min(ROW_TILE, rows)
@@ -49,17 +71,22 @@
             pl.BlockSpec((tile, width), lambda i: (i, 0)),
             pl.BlockSpec((pieces, rank, piece), lambda i: (i, 0, 0)),
             pl.BlockSpec((rank, width), lambda i: (0, 0)),
+            pl.BlockSpec((rank, width), lambda i: (0, 0)),
+            pl.BlockSpec((rank, width), lambda i: (0, 0)),
         ],
         out_specs=[
             pl.BlockSpec((pieces, rank, piece), lambda i: (i, 0, 0)),
-            pl.BlockSpec((rank, width), lambda i: (0, 0)),
+            pl.BlockSpec((rank, steps), lambda i: (0, 0)),
+            pl.BlockSpec((rank, kinds), lambda i: (0, 0)),
         ],
         out_shape=[
             jax.ShapeDtypeStruct((count, rank, piece), jnp.float32),
-            jax.ShapeDtypeStruct((rank, width), jnp.float32),
+            jax.ShapeDtypeStruct((rank, steps), jnp.float32),
+            jax.ShapeDtypeStruct((rank, kinds), jnp.float32),
         ],
+        scratch_shapes=[pltpu.VMEM((rank, width), jnp.float32)],
         compiler_params=pltpu.CompilerParams(dimension_semantics=("arbitrary",)),
-    )(observed, gathered, khatri)
+    )(observed, gathered, khatri, species_wide, time_wide)
 
 
 def gather_blocks(values, axis):
@@ -95,14 +122,11 @@
         .astype(jnp.bfloat16)
     )
     gathered = gather_blocks(node_factor, "tm")
-    blocks, contracted_t = fused(observed, gathered, khatri)
-    column = jnp.arange(flat_width)
-    step_of = (column[:, None] // species == jnp.arange(time_dev)[None, :]).astype(jnp.float32)
-    species_of = (column[:, None] % species == jnp.arange(species)[None, :]).astype(jnp.float32)
     species_wide = jnp.tile(species_vals, (1, time_dev))
     time_wide = jnp.repeat(time_vals, species, axis=1)
-    time_part = jnp.dot(contracted_t * species_wide, step_of, precision=lax.Precision.HIGHEST)
-    species_part = jnp.dot(contracted_t * time_wide, species_of, precision=lax.Precision.HIGHEST)
+    blocks, time_part, species_part = fused(
+        observed, gathered, khatri, species_wide, time_wide, time_dev, species
+    )
 
     small = jnp.concatenate([time_part, species_part], axis=1)
     small_sum = butterfly_sum(small, "node")

time: 88.2 us -> 87.6 us (level)
  starting transfers between devices: 25.4 us -> 29.8 us
  waiting for transfers between devices: 41 us -> 37.1 us
  matrix products: 2.75 us -> 0 us
  other arithmetic: 2.27 us -> 3.86 us
    ppermute x8, starting transfers between devices: 9.87 us -> 14.3 us  [butterfly_sum(): values = values + lax.ppermute(values, axis, pairs)]
    ppermute x8, waiting for transfers between devices: 28.4 us -> 24.6 us  [butterfly_sum(): values = values + lax.ppermute(values, axis, pairs)]
    dot_general x2 -> x0, matrix products: 2.75 us -> none  [the longest x1 1.38 us: shards(): jnp.dot(contracted_t * species_wide, step_of, precision=lax.Precision.HIG...]
  transfers between devices with their start and end apart: 10 -> 10, of which waited for: 9 -> 9; matrix products, arithmetic and copies ran while one was open for 8% -> 7% of each run, Pallas kernels for 0% -> 0%
where the time goes in v8:
time: 87.6 us; the launch traced here: 86.9 us
  waiting for transfers between devices  37.1 us (42%)
  starting transfers between devices  29.8 us (34%)
  Pallas kernels  10.2 us (12%)
  local copies, waits for them, and re-layouts  5.13 us (6%)
  other arithmetic  3.86 us (4%)
    ppermute x8, waiting for transfers between devices, butterfly_sum(): values = values + lax.ppermute(values, axis, pairs)  24.6 us
    ppermute x8, starting transfers between devices, butterfly_sum(): values = values + lax.ppermute(values, axis, pairs)  14.3 us
    all_to_all x1, waiting for transfers between devices, gather_blocks(): return lax.all_to_all(copies, axis, 0, 0, tiled=True)  12.5 us
    pallas_call x1, Pallas kernels, fused(): pl.pallas_call(fused_kernel, grid=(rows // tile,), in_specs=[pl.BlockSpec...  10.2 us
    all_to_all x1, starting transfers between devices, gather_blocks(): return lax.all_to_all(copies, axis, 0, 0, tiled=True)  9.94 us
    all_to_all x1, starting transfers between devices, shards(): summed = lax.all_to_all(blocks, 'tm', 0, 0, tiled=True).sum(0)  5.6 us
  transfers between devices with their start and end apart: 10, of which 9 were waited for; matrix products, arithmetic and copies ran while one was open for 7% of the time, Pallas kernels for 0%

profile of v8, /device:TPU:22, one launch (start us, length us, event | category | flops | bytes accessed | tf_op | source)
XLA Modules:
  0.0 86.9 jit_solution(10801085346223182627)
XLA Ops:
  0.6 1.6 %broadcast_in_dim.2 = bf16[16,64,256]{2,1,0:T(8,128)(2,1)} broadcast(bf16[64,256]{1,0:T(8,128)(2,1)} %param.5), dimensions={1,2} | broadcast | bytes 557056 | tf_op jit(solution)/shard_map/broadcast_in_dim | solution.py:94
  2.2 9.9 %all-to-all-start = ((bf16[16,64,256]{2,1,0:T(8,128)(2,1)}), bf16[16,64,256]{2,1,0:T(8,128)(2,1)S(1)}, u32[]{:S(2)}, u32[]{:S(2)}) async-start(bf16[16,64,256]{2,1,0:T(8,128)(2,1)} %broadcast_in_dim.2), calls=%async_computation | async-start | bytes 1048576 | tf_op jit(solution)/shard_map/all_to_all | solution.py:95
  12.2 0.8 copy.9
  13.0 0.2 copy.10.time_wide_ref
  13.2 0.7 mul.20
  14.0 0.2 copy.11.species_wide_ref
  14.2 0.7 multiply_convert_fusion.khatri_ref
  14.9 12.5 %all-to-all-done.gathered_ref = bf16[16,64,256]{2,1,0:T(8,128)(2,1)S(1)} async-done(((bf16[16,64,256]{2,1,0:T(8,128)(2,1)}), bf16[16,64,256]{2,1,0:T(8,128)(2,1)S(1)}, u32[]{:S(2)}, u32[]{:S(2)}) %all-to-all-start) | async-done | bytes 524320 | tf_op jit(solution)/shard_map/all_to_all | solution.py:95
  27.4 0.8 copy-done.2
  28.3 10.2 %shard_map.67 = (f32[16,64,256]{2,1,0:T(8,128)}, f32[64,64]{1,0:T(8,128)}, f32[64,16]{1,0:T(8,128)}) custom-call(bf16[4096,1024]{1,0:T(8,128)(2,1)} %obs_ref.1, bf16[16,64,256]{2,1,0:T(8,128)(2,1)} %copy-done.2, bf16[64,1024]{1,0:T(8,128)(2,1)} %multiply_convert_fusion.khatri_ref, f32[64,1024]{1,0:T(8,128)} %copy-done.1, f32[64,1024]{1,0:T(8,128)} %copy-done), custom_call_target="tpu_custom_call" | custom-call | tf_op jit(solution)/shard_map/pallas_call | solution.py:67
  38.5 5.6 %all-to-all-start.1 = ((f32[16,64,256]{2,1,0:T(8,128)}), f32[16,64,256]{2,1,0:T(8,128)S(1)}, u32[]{:S(2)}, u32[]{:S(2)}) async-start(f32[16,64,256]{2,1,0:T(8,128)} %get-tuple-element.6), calls=%async_computation.1 | async-start | bytes 2097152 | tf_op jit(solution)/shard_map/all_to_all | solution.py:137
  44.1 0.9 pad_maximum_fusion
  45.0 1.2 %collective-permute-done = f32[64,80]{1,0:T(8,128)S(1)} collective-permute-done((f32[64,80]{1,0:T(8,128)S(1)}, f32[64,80]{1,0:T(8,128)S(1)}, u32[]{:S(2)}, u32[]{:S(2)}) %collective-permute-start) | collective-permute-done | bytes 20512 | tf_op jit(solution)/shard_map/ppermute | solution.py:103
  46.2 0.9 fusion
  47.0 1.4 %collective-permute-start.1 = (f32[64,80]{1,0:T(8,128)S(1)}, f32[64,80]{1,0:T(8,128)S(1)}, u32[]{:S(2)}, u32[]{:S(2)}) collective-permute-start(f32[64,80]{1,0:T(8,128)S(1)} %fusion), channel_id=1, source_target_pairs={{0,32},{16,48},{32,0},{48,16},{64,96},{80,112},{96,64},{112,80},{1... | collective-permute-start | bytes 61448 | tf_op jit(solution)/shard_map/ppermute | solution.py:103
  48.5 4.1 %collective-permute-done.1 = f32[64,80]{1,0:T(8,128)S(1)} collective-permute-done((f32[64,80]{1,0:T(8,128)S(1)}, f32[64,80]{1,0:T(8,128)S(1)}, u32[]{:S(2)}, u32[]{:S(2)}) %collective-permute-start.1) | collective-permute-done | bytes 20512 | tf_op jit(solution)/shard_map/ppermute | solution.py:103
  52.6 1.3 %collective-permute-start.2 = (f32[64,80]{1,0:T(8,128)S(1)}, f32[64,80]{1,0:T(8,128)S(1)}, u32[]{:S(2)}, u32[]{:S(2)}) collective-permute-start(f32[64,80]{1,0:T(8,128)S(1)} %add.25), channel_id=1, source_target_pairs={{0,64},{16,80},{32,96},{48,112},{64,0},{80,16},{96,32},{112,48},{1... | collective-permute-start | bytes 61448 | tf_op jit(solution)/shard_map/ppermute | solution.py:103
  53.9 2.6 %collective-permute-done.2 = f32[64,80]{1,0:T(8,128)S(1)} collective-permute-done((f32[64,80]{1,0:T(8,128)S(1)}, f32[64,80]{1,0:T(8,128)S(1)}, u32[]{:S(2)}, u32[]{:S(2)}) %collective-permute-start.2) | collective-permute-done | bytes 20512 | tf_op jit(solution)/shard_map/ppermute | solution.py:103
  56.5 0.3 collective-permute-start.3
  56.9 5.1 %collective-permute-done.3 = f32[64,80]{1,0:T(8,128)S(1)} collective-permute-done((f32[64,80]{1,0:T(8,128)S(1)}, f32[64,80]{1,0:T(8,128)S(1)}, u32[]{:S(2)}, u32[]{:S(2)}) %collective-permute-start.3) | collective-permute-done | bytes 20512 | tf_op jit(solution)/shard_map/ppermute | solution.py:103
  62.0 0.1 slice.9
  62.0 0.2 collective-permute-start.4
  62.3 4.5 %collective-permute-done.4 = f32[64,16]{1,0:T(8,128)S(1)} collective-permute-done((f32[64,16]{1,0:T(8,128)S(1)}, f32[64,16]{1,0:T(8,128)S(1)}, u32[]{:S(2)}, u32[]{:S(2)}) %collective-permute-start.4) | collective-permute-done | bytes 4128 | tf_op jit(solution)/shard_map/ppermute | solution.py:103
  66.8 3.0 %collective-permute-start.5 = (f32[64,16]{1,0:T(8,128)S(1)}, f32[64,16]{1,0:T(8,128)S(1)}, u32[]{:S(2)}, u32[]{:S(2)}) collective-permute-start(f32[64,16]{1,0:T(8,128)S(1)} %slice_add_fusion), channel_id=1, source_target_pairs={{0,2},{1,3},{2,0},{3,1},{4,6},{5,7},{6,4},{7,5},{8,10},{9,11},{10,... | collective-permute-start | bytes 12296 | tf_op jit(solution)/shard_map/ppermute | solution.py:103
  69.8 1.9 %collective-permute-done.5 = f32[64,16]{1,0:T(8,128)S(1)} collective-permute-done((f32[64,16]{1,0:T(8,128)S(1)}, f32[64,16]{1,0:T(8,128)S(1)}, u32[]{:S(2)}, u32[]{:S(2)}) %collective-permute-start.5) | collective-permute-done | bytes 4128 | tf_op jit(solution)/shard_map/ppermute | solution.py:103
  71.7 4.1 %collective-permute-start.6 = (f32[64,16]{1,0:T(8,128)S(1)}, f32[64,16]{1,0:T(8,128)S(1)}, u32[]{:S(2)}, u32[]{:S(2)}) collective-permute-start(f32[64,16]{1,0:T(8,128)S(1)} %add.29), channel_id=1, source_target_pairs={{0,4},{1,5},{2,6},{3,7},{4,0},{5,1},{6,2},{7,3},{8,12},{9,13},{10,... | collective-permute-start | bytes 12296 | tf_op jit(solution)/shard_map/ppermute | solution.py:103
  75.8 1.9 %collective-permute-done.6 = f32[64,16]{1,0:T(8,128)S(1)} collective-permute-done((f32[64,16]{1,0:T(8,128)S(1)}, f32[64,16]{1,0:T(8,128)S(1)}, u32[]{:S(2)}, u32[]{:S(2)}) %collective-permute-start.6) | collective-permute-done | bytes 4128 | tf_op jit(solution)/shard_map/ppermute | solution.py:103
  77.7 3.9 %collective-permute-start.7 = (f32[64,16]{1,0:T(8,128)S(1)}, f32[64,16]{1,0:T(8,128)S(1)}, u32[]{:S(2)}, u32[]{:S(2)}) collective-permute-start(f32[64,16]{1,0:T(8,128)S(1)} %add.30), channel_id=1, source_target_pairs={{0,8},{1,9},{2,10},{3,11},{4,12},{5,13},{6,14},{7,15},{8,0},{9,1},... | collective-permute-start | bytes 12296 | tf_op jit(solution)/shard_map/ppermute | solution.py:103
  81.6 0.6 slice_multiply_fusion
  82.2 3.3 %collective-permute-done.7 = f32[64,16]{1,0:T(8,128)S(1)} collective-permute-done((f32[64,16]{1,0:T(8,128)S(1)}, f32[64,16]{1,0:T(8,128)S(1)}, u32[]{:S(2)}, u32[]{:S(2)}) %collective-permute-start.7) | collective-permute-done | bytes 4128 | tf_op jit(solution)/shard_map/ppermute | solution.py:103
  85.5 0.7 copy.14
  86.3 0.6 broadcast_multiply_fusion
  (16 shorter events, 0.3 us)
Async XLA Ops:
  2.2 25.2 %all-to-all-start = ((bf16[16,64,256]{2,1,0:T(8,128)(2,1)}), bf16[16,64,256]{2,1,0:T(8,128)(2,1)S(1)}, u32[]{:S(2)}, u32[]{:S(2)}) async-start(bf16[16,64,256]{2,1,0:T(8,128)(2,1)} %broadcast_in_dim.2), calls=%async_computation | async-start | bytes 1048576 | tf_op jit(solution)/shard_map/all_to_all | solution.py:95
  13.2 14.2 %copy-start = (f32[64,1024]{1,0:T(8,128)}, f32[64,1024]{1,0:T(8,128)S(1)}, u32[]{:S(2)}) copy-start(f32[64,1024]{1,0:T(8,128)S(1)} %copy.10.time_wide_ref) | copy-start | bytes 786436
  14.1 13.3 %copy-start.1 = (f32[64,1024]{1,0:T(8,128)}, f32[64,1024]{1,0:T(8,128)S(1)}, u32[]{:S(2)}) copy-start(f32[64,1024]{1,0:T(8,128)S(1)} %copy.11.species_wide_ref) | copy-start | bytes 786436
  27.4 0.8 copy-start.2
  38.5 47.7 %all-to-all-start.1 = ((f32[16,64,256]{2,1,0:T(8,128)}), f32[16,64,256]{2,1,0:T(8,128)S(1)}, u32[]{:S(2)}, u32[]{:S(2)}) async-start(f32[16,64,256]{2,1,0:T(8,128)} %get-tuple-element.6), calls=%async_computation.1 | async-start | bytes 2097152 | tf_op jit(solution)/shard_map/all_to_all | solution.py:137
  44.9 1.2 %collective-permute-start = (f32[64,80]{1,0:T(8,128)S(1)}, f32[64,80]{1,0:T(8,128)S(1)}, u32[]{:S(2)}, u32[]{:S(2)}) collective-permute-start(f32[64,80]{1,0:T(8,128)S(1)} %pad_maximum_fusion), channel_id=1, source_target_pairs={{0,16},{16,0},{32,48},{48,32},{64,80},{80,64},{96,112},{112,96},{1... | collective-permute-start | bytes 61448 | tf_op jit(solution)/shard_map/ppermute | solution.py:103
  47.0 5.6 %collective-permute-start.1 = (f32[64,80]{1,0:T(8,128)S(1)}, f32[64,80]{1,0:T(8,128)S(1)}, u32[]{:S(2)}, u32[]{:S(2)}) collective-permute-start(f32[64,80]{1,0:T(8,128)S(1)} %fusion), channel_id=1, source_target_pairs={{0,32},{16,48},{32,0},{48,16},{64,96},{80,112},{96,64},{112,80},{1... | collective-permute-start | bytes 61448 | tf_op jit(solution)/shard_map/ppermute | solution.py:103
  52.6 3.9 %collective-permute-start.2 = (f32[64,80]{1,0:T(8,128)S(1)}, f32[64,80]{1,0:T(8,128)S(1)}, u32[]{:S(2)}, u32[]{:S(2)}) collective-permute-start(f32[64,80]{1,0:T(8,128)S(1)} %add.25), channel_id=1, source_target_pairs={{0,64},{16,80},{32,96},{48,112},{64,0},{80,16},{96,32},{112,48},{1... | collective-permute-start | bytes 61448 | tf_op jit(solution)/shard_map/ppermute | solution.py:103
  56.5 5.4 %collective-permute-start.3 = (f32[64,80]{1,0:T(8,128)S(1)}, f32[64,80]{1,0:T(8,128)S(1)}, u32[]{:S(2)}, u32[]{:S(2)}) collective-permute-start(f32[64,80]{1,0:T(8,128)S(1)} %add.26), channel_id=1, source_target_pairs={{0,128},{16,144},{32,160},{48,176},{64,192},{80,208},{96,224},{112... | collective-permute-start | bytes 61448 | tf_op jit(solution)/shard_map/ppermute | solution.py:103
  62.0 4.7 %collective-permute-start.4 = (f32[64,16]{1,0:T(8,128)S(1)}, f32[64,16]{1,0:T(8,128)S(1)}, u32[]{:S(2)}, u32[]{:S(2)}) collective-permute-start(f32[64,16]{1,0:T(8,128)S(1)} %slice.9), channel_id=1, source_target_pairs={{0,1},{1,0},{2,3},{3,2},{4,5},{5,4},{6,7},{7,6},{8,9},{9,8},{10,11... | collective-permute-start | bytes 12296 | tf_op jit(solution)/shard_map/ppermute | solution.py:103
  66.8 4.9 %collective-permute-start.5 = (f32[64,16]{1,0:T(8,128)S(1)}, f32[64,16]{1,0:T(8,128)S(1)}, u32[]{:S(2)}, u32[]{:S(2)}) collective-permute-start(f32[64,16]{1,0:T(8,128)S(1)} %slice_add_fusion), channel_id=1, source_target_pairs={{0,2},{1,3},{2,0},{3,1},{4,6},{5,7},{6,4},{7,5},{8,10},{9,11},{10,... | collective-permute-start | bytes 12296 | tf_op jit(solution)/shard_map/ppermute | solution.py:103
  71.7 6.0 %collective-permute-start.6 = (f32[64,16]{1,0:T(8,128)S(1)}, f32[64,16]{1,0:T(8,128)S(1)}, u32[]{:S(2)}, u32[]{:S(2)}) collective-permute-start(f32[64,16]{1,0:T(8,128)S(1)} %add.29), channel_id=1, source_target_pairs={{0,4},{1,5},{2,6},{3,7},{4,0},{5,1},{6,2},{7,3},{8,12},{9,13},{10,... | collective-permute-start | bytes 12296 | tf_op jit(solution)/shard_map/ppermute | solution.py:103
  77.7 7.8 %collective-permute-start.7 = (f32[64,16]{1,0:T(8,128)S(1)}, f32[64,16]{1,0:T(8,128)S(1)}, u32[]{:S(2)}, u32[]{:S(2)}) collective-permute-start(f32[64,16]{1,0:T(8,128)S(1)} %add.30), channel_id=1, source_target_pairs={{0,8},{1,9},{2,10},{3,11},{4,12},{5,13},{6,14},{7,15},{8,0},{9,1},... | collective-permute-start | bytes 12296 | tf_op jit(solution)/shard_map/ppermute | solution.py:103

commit v9 on v6

--- a/solution.py
+++ b/solution.py
@@ -1,3 +1,4 @@
+import functools
 import math
 
 import jax
@@ -10,7 +11,7 @@
 ROW_TILE = 1024
 
 
-def fused_kernel(obs_ref, gathered_ref, khatri_ref, node_ref, contracted_ref):
+def fused_kernel(obs_ref, gathered_ref, khatri_ref, node_ref, contracted_ref, *, node_scale):
     step = pl.program_id(0)
     pieces, _, piece = gathered_ref.shape
     khatri = khatri_ref[...]
@@ -23,7 +24,7 @@
     )
     node = lax.dot_general(
         derivative, khatri, (((1,), (1,)), ((), ())), preferred_element_type=jnp.float32
-    ).T
+    ).T * node_scale
     for c in range(pieces):
         node_ref[c] = node[:, c * piece : (c + 1) * piece]
     part = jnp.dot(factor, derivative, preferred_element_type=jnp.float32)
@@ -37,13 +38,13 @@
         contracted_ref[...] += part
 
 
-def fused(observed, gathered, khatri):
+def fused(observed, gathered, khatri, node_scale):
     rows, width = observed.shape
     count, rank, piece = gathered.shape
     tile = min(ROW_TILE, rows)
     pieces = tile // piece
     return pl.pallas_call(
-        fused_kernel,
+        functools.partial(fused_kernel, node_scale=node_scale),
         grid=(rows // tile,),
         in_specs=[
             pl.BlockSpec((tile, width), lambda i: (i, 0)),
@@ -77,6 +78,11 @@
     return values
 
 
+def exact_scale(count):
+    root = math.sqrt(count)
+    return 1.0 / root if root == 2.0 ** round(math.log2(root)) else None
+
+
 def shards(observed, node_factor, time_factor, species_factor):
     factor_rank = node_factor.shape[0]
     time_vals = time_factor.astype(jnp.float32)
@@ -94,20 +100,29 @@
         .reshape(factor_rank, flat_width)
         .astype(jnp.bfloat16)
     )
+    node_scale = exact_scale(steps_all * species)
+    time_scale = exact_scale(nodes_all * species)
+    species_scale = exact_scale(nodes_all * steps_all)
+    folded = None not in (node_scale, time_scale, species_scale)
+
     gathered = gather_blocks(node_factor, "tm")
-    blocks, contracted_t = fused(observed, gathered, khatri)
+    blocks, contracted_t = fused(observed, gathered, khatri, node_scale if folded else 1.0)
     by_step = contracted_t.reshape(factor_rank, time_dev, species)
     time_part = (by_step * species_vals[:, None, :]).sum(2)
     species_part = (by_step * time_vals[:, :, None]).sum(1)
+    if folded:
+        time_part = time_part * time_scale
+        species_part = species_part * species_scale
 
     small = jnp.concatenate([time_part, species_part], axis=1)
     small_sum = butterfly_sum(small, "node")
-    grad_time = small_sum[:, :time_dev] / math.sqrt(nodes_all * species)
-    species_sum = butterfly_sum(small_sum[:, time_dev:], "tm")
-    grad_species = species_sum / math.sqrt(nodes_all * steps_all)
-
-    summed = lax.all_to_all(blocks, "tm", 0, 0, tiled=True).sum(0)
-    grad_node = summed / math.sqrt(steps_all * species)
+    grad_time = small_sum[:, :time_dev]
+    grad_species = butterfly_sum(small_sum[:, time_dev:], "tm")
+    grad_node = lax.all_to_all(blocks, "tm", 0, 0, tiled=True).sum(0)
+    if not folded:
+        grad_time = grad_time / math.sqrt(nodes_all * species)
+        grad_species = grad_species / math.sqrt(nodes_all * steps_all)
+        grad_node = grad_node / math.sqrt(steps_all * species)
     return (grad_node, grad_time, grad_species)
 
 

time: 85.9 us -> 85.9 us (level)
    div x3 -> x0, other arithmetic: 1.24 us -> none  [the longest x1 0.64 us: shards(): grad_node = summed / math.sqrt(steps_all * species)]
where the time goes in v9:
time: 85.9 us; the launch traced here: 85.5 us
  waiting for transfers between devices  37.9 us (44%)
  starting transfers between devices  28.8 us (34%)
  Pallas kernels  9.98 us (12%)
  local copies, waits for them, and re-layouts  5.82 us (7%)
  other arithmetic  2.32 us (3%)
    ppermute x8, waiting for transfers between devices, butterfly_sum(): values = values + lax.ppermute(values, axis, pairs)  24.9 us
    ppermute x8, starting transfers between devices, butterfly_sum(): values = values + lax.ppermute(values, axis, pairs)  13.3 us
    all_to_all x1, waiting for transfers between devices, gather_blocks(): return lax.all_to_all(copies, axis, 0, 0, tiled=True)  12.9 us
    pallas_call x1, Pallas kernels, fused(): pl.pallas_call(functools.partial(fused_kernel, node_scale=node_scale), gr...  9.98 us
    all_to_all x1, starting transfers between devices, gather_blocks(): return lax.all_to_all(copies, axis, 0, 0, tiled=True)  9.94 us
    all_to_all x1, starting transfers between devices, shards(): grad_node = lax.all_to_all(blocks, 'tm', 0, 0, tiled=True).sum(0)  5.6 us
  transfers between devices with their start and end apart: 10, of which 9 were waited for; matrix products, arithmetic and copies ran while one was open for 6% of the time, Pallas kernels for 0%

profile of v9, /device:TPU:22, one launch (start us, length us, event | category | flops | bytes accessed | tf_op | source)
XLA Modules:
  0.0 85.5 jit_solution(9202828438206747428)
XLA Ops:
  0.6 1.6 %broadcast_in_dim.2 = bf16[16,64,256]{2,1,0:T(8,128)(2,1)} broadcast(bf16[64,256]{1,0:T(8,128)(2,1)} %param.5), dimensions={1,2} | broadcast | bytes 557056 | tf_op jit(solution)/shard_map/broadcast_in_dim | solution.py:68
  2.2 9.9 %all-to-all-start = ((bf16[16,64,256]{2,1,0:T(8,128)(2,1)}), bf16[16,64,256]{2,1,0:T(8,128)(2,1)S(1)}, u32[]{:S(2)}, u32[]{:S(2)}) async-start(bf16[16,64,256]{2,1,0:T(8,128)(2,1)} %broadcast_in_dim.2), calls=%async_computation | async-start | bytes 1048576 | tf_op jit(solution)/shard_map/all_to_all | solution.py:69
  12.2 0.8 copy.9
  13.0 0.7 convert_element_type.12
  13.7 0.1 multiply_convert_fusion
  13.7 0.8 copy.10.khatri_ref
  14.5 12.9 %all-to-all-done.gathered_ref = bf16[16,64,256]{2,1,0:T(8,128)(2,1)S(1)} async-done(((bf16[16,64,256]{2,1,0:T(8,128)(2,1)}), bf16[16,64,256]{2,1,0:T(8,128)(2,1)S(1)}, u32[]{:S(2)}, u32[]{:S(2)}) %all-to-all-start) | async-done | bytes 524320 | tf_op jit(solution)/shard_map/all_to_all | solution.py:69
  27.4 0.8 copy-done
  28.2 10.0 %shard_map.67 = (f32[16,64,256]{2,1,0:T(8,128)}, f32[64,1024]{1,0:T(8,128)}) custom-call(bf16[4096,1024]{1,0:T(8,128)(2,1)} %obs_ref.1, bf16[16,64,256]{2,1,0:T(8,128)(2,1)} %copy-done, bf16[64,1024]{1,0:T(8,128)(2,1)} %copy.10.khatri_ref), custom_call_target="tpu_custom_call" | custom-call | tf_op jit(solution)/shard_map/pallas_call | solution.py:46
  38.2 5.6 %all-to-all-start.1 = ((f32[16,64,256]{2,1,0:T(8,128)}), f32[16,64,256]{2,1,0:T(8,128)S(1)}, u32[]{:S(2)}, u32[]{:S(2)}) async-start(f32[16,64,256]{2,1,0:T(8,128)} %get-tuple-element.5), calls=%async_computation.1 | async-start | bytes 2097152 | tf_op jit(solution)/shard_map/all_to_all | solution.py:121
  43.8 1.1 %copy.11 = f32[64,1024]{0,1:T(8,128)S(1)} copy(f32[64,1024]{1,0:T(8,128)} %get-tuple-element.6) | data formatting | bytes 524288 | tf_op jit(solution)/shard_map/pallas_call | solution.py:46
  44.9 0.1 multiply_reduce_fusion.1
  45.1 0.1 multiply_reduce_fusion
  45.2 0.1 collective-permute-start
  45.3 1.2 %collective-permute-done = f32[64,80]{0,1:T(8,128)S(1)} collective-permute-done((f32[64,80]{0,1:T(8,128)S(1)}, f32[64,80]{0,1:T(8,128)S(1)}, u32[]{:S(2)}, u32[]{:S(2)}) %collective-permute-start) | collective-permute-done | bytes 20512 | tf_op jit(solution)/shard_map/ppermute | solution.py:77
  46.5 1.5 %collective-permute-start.1 = (f32[64,80]{0,1:T(8,128)S(1)}, f32[64,80]{0,1:T(8,128)S(1)}, u32[]{:S(2)}, u32[]{:S(2)}) collective-permute-start(f32[64,80]{0,1:T(8,128)S(1)} %fusion), channel_id=1, source_target_pairs={{0,32},{16,48},{32,0},{48,16},{64,96},{80,112},{96,64},{112,80},{1... | collective-permute-start | bytes 61448 | tf_op jit(solution)/shard_map/ppermute | solution.py:77
  48.0 4.3 %collective-permute-done.1 = f32[64,80]{0,1:T(8,128)S(1)} collective-permute-done((f32[64,80]{0,1:T(8,128)S(1)}, f32[64,80]{0,1:T(8,128)S(1)}, u32[]{:S(2)}, u32[]{:S(2)}) %collective-permute-start.1) | collective-permute-done | bytes 20512 | tf_op jit(solution)/shard_map/ppermute | solution.py:77
  52.3 1.3 %collective-permute-start.2 = (f32[64,80]{0,1:T(8,128)S(1)}, f32[64,80]{0,1:T(8,128)S(1)}, u32[]{:S(2)}, u32[]{:S(2)}) collective-permute-start(f32[64,80]{0,1:T(8,128)S(1)} %add.25), channel_id=1, source_target_pairs={{0,64},{16,80},{32,96},{48,112},{64,0},{80,16},{96,32},{112,48},{1... | collective-permute-start | bytes 61448 | tf_op jit(solution)/shard_map/ppermute | solution.py:77
  53.6 2.7 %collective-permute-done.2 = f32[64,80]{0,1:T(8,128)S(1)} collective-permute-done((f32[64,80]{0,1:T(8,128)S(1)}, f32[64,80]{0,1:T(8,128)S(1)}, u32[]{:S(2)}, u32[]{:S(2)}) %collective-permute-start.2) | collective-permute-done | bytes 20512 | tf_op jit(solution)/shard_map/ppermute | solution.py:77
  56.3 0.3 collective-permute-start.3
  56.7 5.2 %collective-permute-done.3 = f32[64,80]{0,1:T(8,128)S(1)} collective-permute-done((f32[64,80]{0,1:T(8,128)S(1)}, f32[64,80]{0,1:T(8,128)S(1)}, u32[]{:S(2)}, u32[]{:S(2)}) %collective-permute-start.3) | collective-permute-done | bytes 20512 | tf_op jit(solution)/shard_map/ppermute | solution.py:77
  61.8 0.2 collective-permute-start.4
  62.1 4.0 %collective-permute-done.4 = f32[64,16]{0,1:T(8,128)S(1)} collective-permute-done((f32[64,16]{0,1:T(8,128)S(1)}, f32[64,16]{0,1:T(8,128)S(1)}, u32[]{:S(2)}, u32[]{:S(2)}) %collective-permute-start.4) | collective-permute-done | bytes 4128 | tf_op jit(solution)/shard_map/ppermute | solution.py:77
  66.0 2.4 %collective-permute-start.5 = (f32[64,16]{0,1:T(8,128)S(1)}, f32[64,16]{0,1:T(8,128)S(1)}, u32[]{:S(2)}, u32[]{:S(2)}) collective-permute-start(f32[64,16]{0,1:T(8,128)S(1)} %slice_add_fusion), channel_id=1, source_target_pairs={{0,2},{1,3},{2,0},{3,1},{4,6},{5,7},{6,4},{7,5},{8,10},{9,11},{10,... | collective-permute-start | bytes 12296 | tf_op jit(solution)/shard_map/ppermute | solution.py:77
  68.5 1.6 %collective-permute-done.5 = f32[64,16]{0,1:T(8,128)S(1)} collective-permute-done((f32[64,16]{0,1:T(8,128)S(1)}, f32[64,16]{0,1:T(8,128)S(1)}, u32[]{:S(2)}, u32[]{:S(2)}) %collective-permute-start.5) | collective-permute-done | bytes 4128 | tf_op jit(solution)/shard_map/ppermute | solution.py:77
  70.1 4.8 %collective-permute-start.6 = (f32[64,16]{0,1:T(8,128)S(1)}, f32[64,16]{0,1:T(8,128)S(1)}, u32[]{:S(2)}, u32[]{:S(2)}) collective-permute-start(f32[64,16]{0,1:T(8,128)S(1)} %add.29), channel_id=1, source_target_pairs={{0,4},{1,5},{2,6},{3,7},{4,0},{5,1},{6,2},{7,3},{8,12},{9,13},{10,... | collective-permute-start | bytes 12296 | tf_op jit(solution)/shard_map/ppermute | solution.py:77
  74.9 1.7 %collective-permute-done.6 = f32[64,16]{0,1:T(8,128)S(1)} collective-permute-done((f32[64,16]{0,1:T(8,128)S(1)}, f32[64,16]{0,1:T(8,128)S(1)}, u32[]{:S(2)}, u32[]{:S(2)}) %collective-permute-start.6) | collective-permute-done | bytes 4128 | tf_op jit(solution)/shard_map/ppermute | solution.py:77
  76.6 2.6 %collective-permute-start.7 = (f32[64,16]{0,1:T(8,128)S(1)}, f32[64,16]{0,1:T(8,128)S(1)}, u32[]{:S(2)}, u32[]{:S(2)}) collective-permute-start(f32[64,16]{0,1:T(8,128)S(1)} %add.30), channel_id=1, source_target_pairs={{0,8},{1,9},{2,10},{3,11},{4,12},{5,13},{6,14},{7,15},{8,0},{9,1},... | collective-permute-start | bytes 12296 | tf_op jit(solution)/shard_map/ppermute | solution.py:77
  79.2 0.7 copy.12
  79.9 4.3 %collective-permute-done.7 = f32[64,16]{0,1:T(8,128)S(1)} collective-permute-done((f32[64,16]{0,1:T(8,128)S(1)}, f32[64,16]{0,1:T(8,128)S(1)}, u32[]{:S(2)}, u32[]{:S(2)}) %collective-permute-start.7) | collective-permute-done | bytes 4128 | tf_op jit(solution)/shard_map/ppermute | solution.py:77
  84.2 0.6 add.31
  84.8 0.7 reduce_sum.27
  (14 shorter events, 0.1 us)
Async XLA Ops:
  2.2 25.2 %all-to-all-start = ((bf16[16,64,256]{2,1,0:T(8,128)(2,1)}), bf16[16,64,256]{2,1,0:T(8,128)(2,1)S(1)}, u32[]{:S(2)}, u32[]{:S(2)}) async-start(bf16[16,64,256]{2,1,0:T(8,128)(2,1)} %broadcast_in_dim.2), calls=%async_computation | async-start | bytes 1048576 | tf_op jit(solution)/shard_map/all_to_all | solution.py:69
  27.4 0.8 copy-start
  38.2 46.6 %all-to-all-start.1 = ((f32[16,64,256]{2,1,0:T(8,128)}), f32[16,64,256]{2,1,0:T(8,128)S(1)}, u32[]{:S(2)}, u32[]{:S(2)}) async-start(f32[16,64,256]{2,1,0:T(8,128)} %get-tuple-element.5), calls=%async_computation.1 | async-start | bytes 2097152 | tf_op jit(solution)/shard_map/all_to_all | solution.py:121
  45.2 1.3 %collective-permute-start = (f32[64,80]{0,1:T(8,128)S(1)}, f32[64,80]{0,1:T(8,128)S(1)}, u32[]{:S(2)}, u32[]{:S(2)}) collective-permute-start(f32[64,80]{0,1:T(8,128)S(1)} %pad_maximum_fusion), channel_id=1, source_target_pairs={{0,16},{16,0},{32,48},{48,32},{64,80},{80,64},{96,112},{112,96},{1... | collective-permute-start | bytes 61448 | tf_op jit(solution)/shard_map/ppermute | solution.py:77
  46.5 5.8 %collective-permute-start.1 = (f32[64,80]{0,1:T(8,128)S(1)}, f32[64,80]{0,1:T(8,128)S(1)}, u32[]{:S(2)}, u32[]{:S(2)}) collective-permute-start(f32[64,80]{0,1:T(8,128)S(1)} %fusion), channel_id=1, source_target_pairs={{0,32},{16,48},{32,0},{48,16},{64,96},{80,112},{96,64},{112,80},{1... | collective-permute-start | bytes 61448 | tf_op jit(solution)/shard_map/ppermute | solution.py:77
  52.3 4.0 %collective-permute-start.2 = (f32[64,80]{0,1:T(8,128)S(1)}, f32[64,80]{0,1:T(8,128)S(1)}, u32[]{:S(2)}, u32[]{:S(2)}) collective-permute-start(f32[64,80]{0,1:T(8,128)S(1)} %add.25), channel_id=1, source_target_pairs={{0,64},{16,80},{32,96},{48,112},{64,0},{80,16},{96,32},{112,48},{1... | collective-permute-start | bytes 61448 | tf_op jit(solution)/shard_map/ppermute | solution.py:77
  56.3 5.5 %collective-permute-start.3 = (f32[64,80]{0,1:T(8,128)S(1)}, f32[64,80]{0,1:T(8,128)S(1)}, u32[]{:S(2)}, u32[]{:S(2)}) collective-permute-start(f32[64,80]{0,1:T(8,128)S(1)} %add.26), channel_id=1, source_target_pairs={{0,128},{16,144},{32,160},{48,176},{64,192},{80,208},{96,224},{112... | collective-permute-start | bytes 61448 | tf_op jit(solution)/shard_map/ppermute | solution.py:77
  61.8 4.2 %collective-permute-start.4 = (f32[64,16]{0,1:T(8,128)S(1)}, f32[64,16]{0,1:T(8,128)S(1)}, u32[]{:S(2)}, u32[]{:S(2)}) collective-permute-start(f32[64,16]{0,1:T(8,128)S(1)} %slice.9), channel_id=1, source_target_pairs={{0,1},{1,0},{2,3},{3,2},{4,5},{5,4},{6,7},{7,6},{8,9},{9,8},{10,11... | collective-permute-start | bytes 12296 | tf_op jit(solution)/shard_map/ppermute | solution.py:77
  66.0 4.1 %collective-permute-start.5 = (f32[64,16]{0,1:T(8,128)S(1)}, f32[64,16]{0,1:T(8,128)S(1)}, u32[]{:S(2)}, u32[]{:S(2)}) collective-permute-start(f32[64,16]{0,1:T(8,128)S(1)} %slice_add_fusion), channel_id=1, source_target_pairs={{0,2},{1,3},{2,0},{3,1},{4,6},{5,7},{6,4},{7,5},{8,10},{9,11},{10,... | collective-permute-start | bytes 12296 | tf_op jit(solution)/shard_map/ppermute | solution.py:77
  70.1 6.5 %collective-permute-start.6 = (f32[64,16]{0,1:T(8,128)S(1)}, f32[64,16]{0,1:T(8,128)S(1)}, u32[]{:S(2)}, u32[]{:S(2)}) collective-permute-start(f32[64,16]{0,1:T(8,128)S(1)} %add.29), channel_id=1, source_target_pairs={{0,4},{1,5},{2,6},{3,7},{4,0},{5,1},{6,2},{7,3},{8,12},{9,13},{10,... | collective-permute-start | bytes 12296 | tf_op jit(solution)/shard_map/ppermute | solution.py:77
  76.6 7.6 %collective-permute-start.7 = (f32[64,16]{0,1:T(8,128)S(1)}, f32[64,16]{0,1:T(8,128)S(1)}, u32[]{:S(2)}, u32[]{:S(2)}) collective-permute-start(f32[64,16]{0,1:T(8,128)S(1)} %add.30), channel_id=1, source_target_pairs={{0,8},{1,9},{2,10},{3,11},{4,12},{5,13},{6,14},{7,15},{8,0},{9,1},... | collective-permute-start | bytes 12296 | tf_op jit(solution)/shard_map/ppermute | solution.py:77
